TPU v7x, 32 devices: a whole 2x2x4 slice. The times are simulated.
32 devices in a mesh: region: 2 (over x), east: 8 (over z, y), north: 2 (over core).
Axes of the slice: x: 2, y: 2, z: 4, core: 2. Of those that a mesh axis runs over, the one named last changes fastest.
Arguments:
- photos: bfloat16 [1024, 4, 16384], P(('region', 'east', 'north')), parts along dimension 0, may hold values from -6 to 6
- footprint: int32 [1024, 1], P(('region', 'east', 'north')), parts along dimension 0, may hold values from 0 to 15; in each aligned block of 32 rows (0 to 31, 32 to 63, ...) at most 2 rows name the same one
- placement: int32 [1024], P(('region', 'east', 'north')), parts along dimension 0, may hold values from 0 to 15
- mask_rows: int32 [1024, 2], P(('region', 'east', 'north')), parts along dimension 0, may hold values from 0 to 128, as said below
- tile_scale: bfloat16 [1024], P(('region', 'east', 'north')), parts along dimension 0, may hold values from 0.5 to 2
Outputs:
- band_zero: bfloat16 [4, 2048, 4096], P(None, ('region', 'north'), 'east'), parts along dimension 1
- band_one: bfloat16 [4, 1024, 2048], P(None, ('region', 'north'), 'east'), parts along dimension 1
- band_two: bfloat16 [4, 512, 1024], P(None, ('region', 'north'), 'east'), parts along dimension 1
- band_three: bfloat16 [4, 256, 512], P(None, 'region'), parts along dimension 1
- apex: bfloat16 [4, 128, 256], P(None, 'region'), parts along dimension 1
There are 2 independent parts, one for each index of `region`. A program takes and returns all parts, laid end to end along the dimension named above; each array names one. Nothing has to cross between parts.
Inputs may be any that keep to these rules, and one draw needn't show every extreme that they name: `footprint`: among the 32 rows of one device no tile is named more than 2 times. `mask_rows`: each row holds a first row below one past the last row.
All inputs are finite; a program needn't handle non-finite values.
Results may differ from a plain program's by a relative error of at most 0.001.
Values may be sent and summed in bfloat16 or wider, within the bound.
No kernel may reach another device: no remote copies, remote signals or barrier semaphores. Data moves between devices by JAX's collectives and lax.ppermute only.
A program may use at most 128 MiB of HBM per device.

v0:
```python
import jax
import jax.numpy as jnp
from jax import lax
from jax.sharding import PartitionSpec as P

BANDS = 4
PATCH = 128
TILE = 512
CAP = 2
BLOCKS = 16


KERNEL = (0.0625, 0.25, 0.375, 0.25, 0.0625)
FLOOR = 0.1
MARGINS = (22, 10, 4, 1)


def padded_2(block, sides, width):
    for axis, dim in sides:
        count = lax.axis_size(axis)
        forward = [(i, i + 1) for i in range(count - 1)]
        backward = [(target, source) for source, target in forward]
        low = lax.ppermute(
            lax.slice_in_dim(block, block.shape[dim] - width, None, axis=dim), axis, forward
        )
        high = lax.ppermute(lax.slice_in_dim(block, 0, width, axis=dim), axis, backward)
        block = jnp.concatenate([low, block, high], axis=dim)
    return block


def tap_table(offset, scale):
    table = jnp.zeros(offset.shape, jnp.float32)
    for tap_index in range(5):
        table = table + jnp.where(offset == tap_index, scale * KERNEL[tap_index], 0.0)
    return table


def reduce_table(size_in):
    size_out = (size_in - 3) // 2
    out_index = jnp.arange(size_out, dtype=jnp.int32)
    in_index = jnp.arange(size_in, dtype=jnp.int32)
    return tap_table(in_index[None, :] - 2 * out_index[:, None], 1.0)


def expand_table(size_in):
    size_out = 2 * (size_in - 2)
    out_index = jnp.arange(size_out, dtype=jnp.int32)
    in_index = jnp.arange(size_in, dtype=jnp.int32)
    return tap_table(2 * in_index[None, :] - out_index[:, None], 2.0)


def apply_tables(padded, row_table, col_table):
    rows_done = jnp.einsum(
        "ih,chw->ciw",
        row_table,
        padded,
        precision=lax.Precision.HIGHEST,
        preferred_element_type=jnp.float32,
    )
    return jnp.einsum(
        "ciw,jw->cij",
        rows_done,
        col_table,
        precision=lax.Precision.HIGHEST,
        preferred_element_type=jnp.float32,
    )


def reduce_padded(padded):
    return apply_tables(padded, reduce_table(padded.shape[1]), reduce_table(padded.shape[2]))


def expand_padded(padded):
    return apply_tables(padded, expand_table(padded.shape[1]), expand_table(padded.shape[2]))


def normalize(grid_field):
    return grid_field[:-1] / jnp.maximum(grid_field[-1:], FLOOR)


def crop_margin(grid_field, margin, keep):
    cut = margin - keep
    return grid_field[:, cut : grid_field.shape[1] - cut, cut : grid_field.shape[2] - cut]


def mask_region(grid_field, margin, tile_side, north_pos, east_pos, north_count, east_count):
    row_global = north_pos * tile_side + jnp.arange(grid_field.shape[1], dtype=jnp.int32) - margin
    col_global = east_pos * tile_side + jnp.arange(grid_field.shape[2], dtype=jnp.int32) - margin
    row_keep = (row_global >= 0) & (row_global < north_count * tile_side)
    col_keep = (col_global >= 0) & (col_global < east_count * tile_side)
    keep_table = (row_keep[:, None] & col_keep[None, :]).astype(jnp.float32)
    return grid_field * keep_table[None, :, :]


def body(photos, footprint, placement, mask_rows, tile_scale):
    east_count = lax.axis_size("east")
    north_count = lax.axis_size("north")
    owners = east_count * north_count
    photo_count = photos.shape[0]
    slot_total = owners * CAP
    target = footprint[:, 0]
    member_table = (target[:, None] == jnp.arange(owners, dtype=jnp.int32)[None, :]).astype(
        jnp.int32
    )
    earlier_count = jnp.cumsum(member_table, axis=0) - member_table
    place_rank = jnp.sum(earlier_count * member_table, axis=1)
    slot_index = target * CAP + place_rank
    slot_match = slot_index[None, :] == jnp.arange(slot_total, dtype=jnp.int32)[:, None]
    filled = jnp.any(slot_match, axis=1)
    source = jnp.sum(
        jnp.where(slot_match, jnp.arange(photo_count, dtype=jnp.int32)[None, :], 0), axis=1
    )
    record = jnp.stack(
        [
            tile_scale.astype(jnp.float32),
            placement.astype(jnp.float32),
            mask_rows[:, 0].astype(jnp.float32),
            mask_rows[:, 1].astype(jnp.float32),
            jnp.ones((photo_count,), jnp.float32),
        ],
        axis=1,
    ).astype(jnp.bfloat16)
    send_photos = jnp.where(filled[:, None, None], photos[source], jnp.zeros((), jnp.bfloat16))
    send_record = jnp.where(filled[:, None], record[source], jnp.zeros((), jnp.bfloat16))
    got_photos, got_record = (
        lax.all_to_all(send_photos, ("east", "north"), split_axis=0, concat_axis=0, tiled=True),
        lax.all_to_all(send_record, ("east", "north"), split_axis=0, concat_axis=0, tiled=True),
    )
    record_value = got_record.astype(jnp.float32)
    gain_scale = record_value[:, 0]
    block_index = record_value[:, 1].astype(jnp.int32)
    lower_row = record_value[:, 2:3]
    upper_row = record_value[:, 3:4]
    live_flag = record_value[:, 4]
    side_index = jnp.arange(PATCH, dtype=jnp.int32)
    edge_weight = (1 + jnp.minimum(side_index, PATCH - 1 - side_index)).astype(jnp.float32)
    feather = edge_weight[:, None] * edge_weight[None, :] / float((PATCH // 2) ** 2)
    side_float = side_index.astype(jnp.float32)
    inside = ((side_float[None, :] >= lower_row) & (side_float[None, :] < upper_row)).astype(
        jnp.float32
    ) * live_flag[:, None]
    weight = inside[:, :, None] * feather[None, :, :]
    gain_value = gain_scale[:, None, None] * weight
    window_photos = got_photos.reshape(slot_total, BANDS, PATCH, PATCH)
    weighted = window_photos.astype(jnp.float32) * gain_value[:, None, :, :]
    block_match = (block_index[None, :] == jnp.arange(BLOCKS, dtype=jnp.int32)[:, None]).astype(
        jnp.float32
    )
    band_sums = jnp.einsum(
        "bk,kcrs->bcrs",
        block_match,
        weighted,
        precision=lax.Precision.HIGHEST,
        preferred_element_type=jnp.float32,
    )
    weight_sums = jnp.einsum(
        "bk,krs->brs",
        block_match,
        weight,
        precision=lax.Precision.HIGHEST,
        preferred_element_type=jnp.float32,
    )
    summed = jnp.concatenate([band_sums, weight_sums[:, None]], axis=1)
    side_blocks = TILE // PATCH
    strips = []
    for block_row in range(side_blocks):
        strips.append(
            jnp.concatenate(
                [summed[block_row * side_blocks + block_col] for block_col in range(side_blocks)],
                axis=2,
            )
        )
    canvas = jnp.concatenate(strips, axis=1)
    results = []
    east_pos = lax.axis_index("east")
    north_pos = lax.axis_index("north")
    grown = padded_2(canvas, (("east", 2), ("north", 1)), MARGINS[0])
    for depth_step in range(3):
        margin_now = MARGINS[depth_step]
        margin_next = MARGINS[depth_step + 1]
        coarse = reduce_padded(grown)
        coarse = mask_region(
            coarse,
            margin_next,
            TILE >> depth_step + 1,
            north_pos,
            east_pos,
            north_count,
            east_count,
        )
        own_field = crop_margin(grown, margin_now, 0)
        coarse_normal = normalize(crop_margin(coarse, margin_next, 1))
        laplace_band = normalize(own_field) - expand_padded(coarse_normal)
        results.append(laplace_band.astype(jnp.bfloat16))
        grown = coarse
    level_field = crop_margin(grown, MARGINS[3], 0)
    stacked = lax.all_gather(level_field[None], ("east", "north"), axis=0, tiled=True)
    chan_count, tall_size, wide_size = level_field.shape
    whole_field = stacked.reshape(east_count, north_count, chan_count, tall_size, wide_size)
    whole_field = whole_field.transpose(2, 1, 3, 0, 4).reshape(
        chan_count, north_count * tall_size, east_count * wide_size
    )
    top_field = reduce_padded(jnp.pad(whole_field, ((0, 0), (2, 2), (2, 2))))
    top_normal = normalize(top_field)
    band_three = (
        normalize(whole_field) - expand_padded(jnp.pad(top_normal, ((0, 0), (1, 1), (1, 1))))
    ).astype(jnp.bfloat16)
    apex = top_normal.astype(jnp.bfloat16)
    return (results[0], results[1], results[2], band_three, apex)


def solution(mesh):
    return jax.shard_map(
        body,
        mesh=mesh,
        in_specs=(
            P(("region", "east", "north"), None, None),
            P(("region", "east", "north"), None),
            P(("region", "east", "north")),
            P(("region", "east", "north"), None),
            P(("region", "east", "north")),
        ),
        out_specs=(
            P(None, ("region", "north"), "east"),
            P(None, ("region", "north"), "east"),
            P(None, ("region", "north"), "east"),
            P(None, "region", None),
            P(None, "region", None),
        ),
        check_vma=False,
    )
```

profile of v0, /device:TPU:0, one launch (start us, length us, event | category | flops | bytes accessed | tf_op | source)
XLA Modules:
  0.0 301.0 jit_solution(17203847547347885743)
XLA Ops:
  13.3 7.4 %all-to-all-start = ((bf16[16,2,5]{2,1,0:T(2,128)(2,1)}), bf16[16,2,5]{2,1,0:T(2,128)(2,1)S(1)}, u32[]{:S(2)}, u32[]{:S(2)}) async-start(bf16[16,2,5]{2,1,0:T(2,128)(2,1)} %broadcast_select_fusion.1), calls=%async_computation | async-start | bytes 16384 | tf_op jit(solution)/shard_map/all_to_all | solution.py:127
  20.7 8.0 %gather_fusion.1 = bf16[32,4,16384]{2,1,0:T(4,128)(2,1)} fusion(bf16[32,4,16384]{2,1,0:T(4,128)(2,1)} %param.5, s32[1024]{0:T(1024)S(1)} %pad_clamp_fusion), kind=kCustom, calls=%fused_computation.1 | custom fusion | bytes 8388736 | tf_op jit(solution)/shard_map/gather | solution.py:123
  28.7 5.9 %broadcast_select_fusion = bf16[32,4,16384]{2,1,0:T(4,128)(2,1)} fusion(bf16[32,4,16384]{2,1,0:T(4,128)(2,1)} %gather_fusion.1, pred[32]{0:T(512)(128)(4,1)S(1)} %fusion.201), kind=kLoop, calls=%fused_computation.80 | loop fusion | flops 2097152 | bytes 8388640 | tf_op jit(solution)/shard_map/jit(_where)/select_n | solution.py:123
  34.6 6.1 %all-to-all-start.1 = ((bf16[32,4,16384]{2,1,0:T(4,128)(2,1)}), bf16[32,4,16384]{2,1,0:T(4,128)(2,1)}, u32[]{:S(2)}, u32[]{:S(2)}) async-start(bf16[32,4,16384]{2,1,0:T(4,128)(2,1)} %broadcast_select_fusion), calls=%async_computation.1 | async-start | bytes 8388608 | tf_op jit(solution)/shard_map/all_to_all | solution.py:126
  42.6 2.1 fusion.58
  45.3 73.0 %all-to-all-done.1 = bf16[32,4,16384]{2,1,0:T(4,128)(2,1)} async-done(((bf16[32,4,16384]{2,1,0:T(4,128)(2,1)}), bf16[32,4,16384]{2,1,0:T(4,128)(2,1)}, u32[]{:S(2)}, u32[]{:S(2)}) %all-to-all-start.1) | async-done | bytes 4194336 | tf_op jit(solution)/shard_map/all_to_all | solution.py:126
  118.3 8.9 %reshape.371 = f32[32,4,128,128]{3,2,1,0:T(8,128)} reshape(bf16[32,4,16384]{2,1,0:T(4,128)(2,1)} %all-to-all-done.1) | data formatting | bytes 12582912 | tf_op jit(solution)/shard_map/convert_element_type | solution.py:145
  127.3 10.9 %fusion = f32[16,4,128,128]{3,0,2,1:T(8,128)S(1)} fusion(f32[32,4,128,128]{3,2,1,0:T(8,128)} %reshape.371, f32[32,128,128]{2,0,1:T(8,128)S(1)} %multiply_multiply_fusion, s32[32]{0:T(128)S(1)} %fusion.200), kind=kOutput, calls=%fused_computation.18 | convolution fusion | flops 404750848 | bytes 14680192 | tf_op jit(solution)/shard_map/bk,kcrs->bcrs/dot_general | solution.py:149
  138.2 2.8 fusion.110
  140.9 2.7 fusion.119
  143.8 1.7 maximum_maximum_fusion.2
  146.6 2.4 copy.121
  149.0 8.8 %collective-permute-start = (f32[5,512,22]{1,2,0:T(8,128)}, f32[5,512,22]{1,2,0:T(8,128)}, u32[]{:S(2)}, u32[]{:S(2)}) collective-permute-start(f32[5,512,22]{1,2,0:T(8,128)} %copy.121), channel_id=1, source_target_pairs={{0,2},{2,4},{4,6},{6,8},{8,10},{10,12},{12,14},{1,3},{3,5},{5,7},{... | collective-permute-start | bytes 675848 | tf_op jit(solution)/shard_map/ppermute | solution.py:23
  157.8 2.4 copy.122
  161.6 2.0 collective-permute-done
  163.5 2.5 copy.123
  166.0 11.5 %collective-permute-done.1 = f32[5,512,22]{1,2,0:T(8,128)} collective-permute-done((f32[5,512,22]{1,2,0:T(8,128)}, f32[5,512,22]{1,2,0:T(8,128)}, u32[]{:S(2)}, u32[]{:S(2)}) %collective-permute-start.1) | collective-permute-done | bytes 225312 | tf_op jit(solution)/shard_map/ppermute | solution.py:26
  177.5 2.4 copy.124
  179.9 12.6 %pad_maximum_fusion = f32[5,512,556]{2,1,0:T(8,128)S(1)} fusion(f32[5,512,22]{2,1,0:T(8,128)} %copy.124, f32[5,128,128]{2,1,0:T(8,128)} %bitcast.251, f32[5,128,128]{2,1,0:T(8,128)} %bitcast.257, f32[5,128,128]{2,1,0:T(8,128)} %bitcast.245, f32[5,128,128]{2,1,0:T(8,128)} %bitcast.239, f32[5,128,128]{2,1,0:T(8,128)} %bitcast.233, ...), kind=kLoop, calls=%fused_computation.74 | loop fusion | flops 24197120 | bytes 11386880 | tf_op jit(solution)/shard_map/concatenate | solution.py:27
  195.3 3.5 %maximum_maximum_fusion = f32[5,512,512]{2,1,0:T(8,128)} fusion(f32[5,128,128]{2,1,0:T(8,128)S(1)} %bitcast.252, f32[5,128,128]{2,1,0:T(8,128)S(1)} %bitcast.258, f32[5,128,128]{2,1,0:T(8,128)S(1)} %bitcast.246, f32[5,128,128]{2,1,0:T(8,128)S(1)} %bitcast.240, f32[5,128,128]{2,1,0:T(8,128)S(1)} %bitcast.234, f32[5,128,128]{2,1,0:T(8,128)S(1)} %bitcast.228, ...), kind=kLoop, calls=%fused_computation.75 | loop fusion | flops 19660800 | bytes 10485760 | tf_op jit(solution)/shard_map/concatenate | solution.py:173
  201.0 12.4 %fusion.1 = f32[5,556,276]{1,2,0:T(8,128)S(1)} fusion(f32[5,22,556]{2,1,0:T(8,128)S(1)} %collective-permute-done.3, f32[5,512,22]{2,1,0:T(8,128)S(1)} %copy-done.15, f32[5,128,128]{2,1,0:T(8,128)S(1)} %bitcast.254, f32[5,128,128]{2,1,0:T(8,128)S(1)} %bitcast.260, f32[5,128,128]{2,1,0:T(8,128)S(1)} %bitcast.248, f32[5,128,128]{2,1,0:T(8,128)S(1)} %bitcast.242, ...), kind=kOutput, calls=%fused_computation.34 | convolution fusion | flops 5150962176 | bytes 9252944 | tf_op jit(solution)/shard_map/ih,chw->ciw/dot_general | solution.py:53
  213.4 7.4 %fusion.54 = f32[5,276,276]{2,1,0:T(8,128)S(1)} fusion(f32[5,556,276]{1,2,0:T(8,128)S(1)} %fusion.1, f32[276,276]{1,0:T(8,128)S(1)} %copy-done.17, s32[276]{0:T(512)S(1)} %iota_multiply_fusion.1), kind=kOutput, calls=%fused_computation.91 | convolution fusion | flops 2543913984 | bytes 4898448 | tf_op jit(solution)/shard_map/ciw,jw->cij/dot_general | solution.py:60
  220.8 2.3 convolution_bitcast_fusion
  224.4 1.7 convolution_bitcast_fusion.3
  232.1 2.9 fusion.64
  235.0 4.5 %fusion.57 = f32[4,258,512]{2,1,0:T(8,128)S(1)} fusion(f32[5,276,276]{2,1,0:T(8,128)S(1)} %fusion.54, f32[258,258]{1,0:T(8,128)S(1)} %fusion.108, s32[258]{0:T(512)S(1)} %iota_multiply_fusion), kind=kOutput, calls=%fused_computation.93 | convolution fusion | flops 1638124544 | bytes 4143104 | tf_op jit(solution)/shard_map/ih,chw->ciw/dot_general | solution.py:53
  239.6 9.1 %fusion.42 = bf16[4,512,512]{2,1,0:T(8,128)(2,1)} fusion(f32[5,512,512]{2,1,0:T(8,128)S(1)} %bitcast.262, f32[512,512]{1,0:T(8,128)S(1)} %copy-done.18, f32[4,258,512]{2,1,0:T(8,128)S(1)} %fusion.57, s32[258]{0:T(512)S(1)} %iota_multiply_fusion), kind=kOutput, calls=%fused_computation.78 | convolution fusion | flops 3251518464 | bytes 9454600 | tf_op jit(solution)/shard_map/ciw,jw->cij/dot_general | solution.py:60
  248.7 26.4 %all-gather.3.cloned.1.call-done = f32[80,64,64]{2,1,0:T(8,128)} async-done(((f32[5,64,64]{2,1,0:T(8,128)}), f32[80,64,64]{2,1,0:T(8,128)}) %all-gather.3.cloned.1.call-update) | async-done | bytes 1310736 | tf_op jit(solution)/shard_map/all_gather | solution.py:197
  275.1 3.4 %copy.153 = f32[8,2,5,64,64]{4,0,3,1,2:T(8,128)S(1)} copy(f32[8,2,5,64,64]{4,3,2,1,0:T(8,128)} %bitcast.263) | data formatting | bytes 2621440 | tf_op jit(solution)/shard_map/reshape | solution.py:199
  278.5 1.7 reshape.369
  285.5 2.2 convolution_bitcast_fusion.2
  289.3 4.4 %fusion.65 = bf16[4,128,512]{2,1,0:T(8,128)(2,1)} fusion(f32[4,128,258]{1,2,0:T(8,128)} %convolution_bitcast_fusion.2, f32[4,128,512]{2,1,0:T(8,128)} %slice.198, f32[128,512]{1,0:T(8,128)S(1)} %max.70, s32[258]{0:T(512)S(1)} %iota_multiply_fusion), kind=kOutput, calls=%fused_computation.102 | convolution fusion | flops 814365696 | bytes 2364424 | tf_op jit(solution)/shard_map/ciw,jw->cij/dot_general | solution.py:60
  (110 shorter events, 30.0 us)
Async XLA Ops:
  13.3 21.3 %all-to-all-start = ((bf16[16,2,5]{2,1,0:T(2,128)(2,1)}), bf16[16,2,5]{2,1,0:T(2,128)(2,1)S(1)}, u32[]{:S(2)}, u32[]{:S(2)}) async-start(bf16[16,2,5]{2,1,0:T(2,128)(2,1)} %broadcast_select_fusion.1), calls=%async_computation | async-start | bytes 16384 | tf_op jit(solution)/shard_map/all_to_all | solution.py:127
  34.6 83.7 %all-to-all-start.1 = ((bf16[32,4,16384]{2,1,0:T(4,128)(2,1)}), bf16[32,4,16384]{2,1,0:T(4,128)(2,1)}, u32[]{:S(2)}, u32[]{:S(2)}) async-start(bf16[32,4,16384]{2,1,0:T(4,128)(2,1)} %broadcast_select_fusion), calls=%async_computation.1 | async-start | bytes 8388608 | tf_op jit(solution)/shard_map/all_to_all | solution.py:126
  40.7 234.4 %all-gather.3.cloned.1.call-start = ((), (), s32[]{:S(2)}) async-start(), calls=%async_computation.2 | async-start | bytes 2785280 | tf_op jit(solution)/shard_map/all_gather | solution.py:197
  127.3 10.9 %copy-start.12 = (f32[16,1,128,128]{3,0,2,1:T(8,128)S(1)}, f32[16,1,128,128]{3,0,2,1:T(8,128)}, u32[]{:S(2)}) copy-start(f32[16,1,128,128]{3,0,2,1:T(8,128)} %fusion.58) | copy-start | bytes 3145732
  143.7 1.7 copy-start
  143.7 1.7 copy-start.2
  143.7 1.7 copy-start.4
  143.7 1.7 copy-start.6
  143.7 1.7 copy-start.8
  143.7 1.7 copy-start.10
  149.0 14.5 %collective-permute-start = (f32[5,512,22]{1,2,0:T(8,128)}, f32[5,512,22]{1,2,0:T(8,128)}, u32[]{:S(2)}, u32[]{:S(2)}) collective-permute-start(f32[5,512,22]{1,2,0:T(8,128)} %copy.121), channel_id=1, source_target_pairs={{0,2},{2,4},{4,6},{6,8},{8,10},{10,12},{12,14},{1,3},{3,5},{5,7},{... | collective-permute-start | bytes 675848 | tf_op jit(solution)/shard_map/ppermute | solution.py:23
  160.2 17.3 %collective-permute-start.1 = (f32[5,512,22]{1,2,0:T(8,128)}, f32[5,512,22]{1,2,0:T(8,128)}, u32[]{:S(2)}, u32[]{:S(2)}) collective-permute-start(f32[5,512,22]{1,2,0:T(8,128)} %copy.122), channel_id=1, source_target_pairs={{2,0},{4,2},{6,4},{8,6},{10,8},{12,10},{14,12},{3,1},{5,3},{7,5},{... | collective-permute-start | bytes 675848 | tf_op jit(solution)/shard_map/ppermute | solution.py:26
  179.9 15.4 %copy-start.1 = (f32[1,5,128,128]{3,0,2,1:T(1,128)S(1)}, f32[1,5,128,128]{3,0,2,1:T(1,128)}, u32[]{:S(2)}) copy-start(f32[1,5,128,128]{3,0,2,1:T(1,128)} %copy-done) | copy-start | bytes 983044
  179.9 15.4 %copy-start.3 = (f32[1,5,128,128]{3,0,2,1:T(1,128)S(1)}, f32[1,5,128,128]{3,0,2,1:T(1,128)}, u32[]{:S(2)}) copy-start(f32[1,5,128,128]{3,0,2,1:T(1,128)} %copy-done.2) | copy-start | bytes 983044
  179.9 15.4 %copy-start.5 = (f32[1,5,128,128]{3,0,2,1:T(1,128)S(1)}, f32[1,5,128,128]{3,0,2,1:T(1,128)}, u32[]{:S(2)}) copy-start(f32[1,5,128,128]{3,0,2,1:T(1,128)} %copy-done.4) | copy-start | bytes 983044
  179.9 15.4 %copy-start.7 = (f32[1,5,128,128]{3,0,2,1:T(1,128)S(1)}, f32[1,5,128,128]{3,0,2,1:T(1,128)}, u32[]{:S(2)}) copy-start(f32[1,5,128,128]{3,0,2,1:T(1,128)} %copy-done.6) | copy-start | bytes 983044
  179.9 15.4 %copy-start.9 = (f32[1,5,128,128]{3,0,2,1:T(1,128)S(1)}, f32[1,5,128,128]{3,0,2,1:T(1,128)}, u32[]{:S(2)}) copy-start(f32[1,5,128,128]{3,0,2,1:T(1,128)} %copy-done.8) | copy-start | bytes 983044
  179.9 15.4 %copy-start.11 = (f32[1,5,128,128]{3,0,2,1:T(1,128)S(1)}, f32[1,5,128,128]{3,0,2,1:T(1,128)}, u32[]{:S(2)}) copy-start(f32[1,5,128,128]{3,0,2,1:T(1,128)} %copy-done.10) | copy-start | bytes 983044
  192.7 7.5 %collective-permute-start.2 = (f32[5,22,556]{2,1,0:T(8,128)S(1)}, f32[5,22,556]{2,1,0:T(8,128)S(1)}, u32[]{:S(2)}, u32[]{:S(2)}) collective-permute-start(f32[5,22,556]{2,1,0:T(8,128)S(1)} %get-tuple-element.11), channel_id=1, source_target_pairs={{0,1},{2,3},{4,5},{6,7},{8,9},{10,11},{12,13},{14,15},{16,17},{18,... | collective-permute-start | bytes 733928 | tf_op jit(solution)/shard_map/ppermute | solution.py:23
  194.0 6.1 %collective-permute-start.3 = (f32[5,22,556]{2,1,0:T(8,128)S(1)}, f32[5,22,556]{2,1,0:T(8,128)S(1)}, u32[]{:S(2)}, u32[]{:S(2)}) collective-permute-start(f32[5,22,556]{2,1,0:T(8,128)S(1)} %get-tuple-element.12), channel_id=1, source_target_pairs={{1,0},{3,2},{5,4},{7,6},{9,8},{11,10},{13,12},{15,14},{17,16},{19,... | collective-permute-start | bytes 733928 | tf_op jit(solution)/shard_map/ppermute | solution.py:26
  198.9 1.7 copy-start.14
  198.9 2.1 copy-start.15
  200.1 13.2 %copy-start.17 = (f32[276,276]{1,0:T(8,128)S(1)}, f32[276,276]{1,0:T(8,128)}, u32[]{:S(2)}) copy-start(f32[276,276]{1,0:T(8,128)} %and_convert_fusion) | copy-start | bytes 914116
  232.1 7.4 %slice-start = ((s8[5242880]{0:T(1024)(128)(4,1)}), s8[4194304]{0:T(1024)(128)(4,1)S(1)}, s32[]{:S(2)}) async-start(s8[5242880]{0:T(1024)(128)(4,1)} %bitcast.261), calls=%async_computation.3 | async-start | bytes 8388608
  235.0 4.6 %slice-start.1 = ((s8[5242880]{0:T(1024)(128)(4,1)}), s8[1048576]{0:T(1024)(128)(4,1)S(1)}, s32[]{:S(2)}) async-start(s8[5242880]{0:T(1024)(128)(4,1)} %bitcast.261), calls=%async_computation.4 | async-start | bytes 2097152
  235.0 4.6 %copy-start.18 = (f32[512,512]{1,0:T(8,128)S(1)}, f32[512,512]{1,0:T(8,128)}, u32[]{:S(2)}) copy-start(f32[512,512]{1,0:T(8,128)} %fusion.67) | copy-start | bytes 3145732
  280.1 1.9 copy-start.16
  282.0 5.7 %copy-start.13 = (f32[4,2,64,8,64]{4,3,2,1,0:T(8,128)S(1)}, f32[4,2,64,8,64]{4,3,2,1,0:T(8,128)}, u32[]{:S(2)}) copy-start(f32[4,2,64,8,64]{4,3,2,1,0:T(8,128)} %slice.255) | copy-start | bytes 3145732
Sparse Core Ops, SparseCore 0:
  228.6 46.4 all-gather.2
where the time goes:
time: 306 us; the launch traced here: 301 us
  waiting for transfers between devices  113 us (37%)
  matrix products  68.6 us (22%)
  other arithmetic  39.6 us (13%)
  local copies, waits for them, and re-layouts  38.5 us (13%)
  starting transfers between devices  26.4 us (9%)
  between operations  15 us (5%)
    all_to_all x1, waiting for transfers between devices, body(): lax.all_to_all(send_photos, ('east', 'north'), split_axis=0, concat_axis=...  73 us
    dot_general x8, matrix products, apply_tables(): jnp.einsum('ciw,jw->cij', rows_done, col_table, precision=lax.Precision.H...  28.9 us
    dot_general x8, matrix products, apply_tables(): jnp.einsum('ih,chw->ciw', row_table, padded, precision=lax.Precision.HIGH...  26.7 us
    all_gather x1, waiting for transfers between devices, body(): lax.all_gather(level_field[None], ('east', 'north'), axis=0, tiled=True)  26.4 us
    concatenate x1, other arithmetic, padded_2(): block = jnp.concatenate([low, block, high], axis=dim)  12.6 us
    ppermute x2, waiting for transfers between devices, padded_2(): lax.ppermute(lax.slice_in_dim(block, 0, width, axis=dim), axis, backward)  11.5 us
    dot_general x1, matrix products, body(): jnp.einsum('bk,kcrs->bcrs', block_match, weighted, precision=lax.Precisio...  10.9 us
    ppermute x2, starting transfers between devices, padded_2(): lax.ppermute(lax.slice_in_dim(block, block.shape[dim] - width, None, axis...  10.1 us
  transfers between devices with their start and end apart: 7, of which 4 were waited for; matrix products, arithmetic and copies ran while one was open for 16% of the time, Pallas kernels for 0%

commit v1 on v0

--- a/solution.py
+++ b/solution.py
@@ -32,7 +32,19 @@
     table = jnp.zeros(offset.shape, jnp.float32)
     for tap_index in range(5):
         table = table + jnp.where(offset == tap_index, scale * KERNEL[tap_index], 0.0)
-    return table
+    return table.astype(jnp.bfloat16)
+
+
+def split_einsum(spec, first, second, table_first):
+    field = second if table_first else first
+    spread_field = field * 65537.0
+    high = spread_field - (spread_field - field)
+    low = field - high
+    both = jnp.concatenate([high, low], axis=0).astype(jnp.bfloat16)
+    pair = (first, both) if table_first else (both, second)
+    term = jnp.einsum(spec, *pair, preferred_element_type=jnp.float32)
+    chan_count = field.shape[0]
+    return term[:chan_count] + term[chan_count:]
 
 
 def reduce_table(size_in):
@@ -50,20 +62,8 @@
 
 
 def apply_tables(padded, row_table, col_table):
-    rows_done = jnp.einsum(
-        "ih,chw->ciw",
-        row_table,
-        padded,
-        precision=lax.Precision.HIGHEST,
-        preferred_element_type=jnp.float32,
-    )
-    return jnp.einsum(
-        "ciw,jw->cij",
-        rows_done,
-        col_table,
-        precision=lax.Precision.HIGHEST,
-        preferred_element_type=jnp.float32,
-    )
+    rows_done = split_einsum("ih,chw->ciw", row_table, padded, True)
+    return split_einsum("ciw,jw->cij", rows_done, col_table, False)
 
 
 def reduce_padded(padded):
@@ -120,13 +120,21 @@
         ],
         axis=1,
     ).astype(jnp.bfloat16)
-    send_photos = jnp.where(filled[:, None, None], photos[source], jnp.zeros((), jnp.bfloat16))
-    send_record = jnp.where(filled[:, None], record[source], jnp.zeros((), jnp.bfloat16))
-    got_photos, got_record = (
-        lax.all_to_all(send_photos, ("east", "north"), split_axis=0, concat_axis=0, tiled=True),
-        lax.all_to_all(send_record, ("east", "north"), split_axis=0, concat_axis=0, tiled=True),
-    )
-    record_value = got_record.astype(jnp.float32)
+    pixel_total = BANDS * PATCH * PATCH
+    payload = jnp.concatenate(
+        [
+            photos.reshape(photo_count, pixel_total),
+            jnp.pad(record, ((0, 0), (0, PATCH - record.shape[1]))),
+        ],
+        axis=1,
+    )
+    pick = slot_match.astype(jnp.bfloat16)
+    send = jnp.einsum("sp,pj->sj", pick, payload, preferred_element_type=jnp.float32).astype(
+        jnp.bfloat16
+    )
+    got = lax.all_to_all(send, ("east", "north"), split_axis=0, concat_axis=0, tiled=True)
+    got_photos = got[:, :pixel_total]
+    record_value = got[:, pixel_total : pixel_total + 5].astype(jnp.float32)
     gain_scale = record_value[:, 0]
     block_index = record_value[:, 1].astype(jnp.int32)
     lower_row = record_value[:, 2:3]
@@ -174,27 +182,27 @@
     results = []
     east_pos = lax.axis_index("east")
     north_pos = lax.axis_index("north")
-    grown = padded_2(canvas, (("east", 2), ("north", 1)), MARGINS[0])
+    levels = [padded_2(canvas, (("east", 2), ("north", 1)), MARGINS[0])]
     for depth_step in range(3):
-        margin_now = MARGINS[depth_step]
-        margin_next = MARGINS[depth_step + 1]
-        coarse = reduce_padded(grown)
-        coarse = mask_region(
-            coarse,
-            margin_next,
-            TILE >> depth_step + 1,
-            north_pos,
-            east_pos,
-            north_count,
-            east_count,
+        coarse = reduce_padded(levels[-1])
+        levels.append(
+            mask_region(
+                coarse,
+                MARGINS[depth_step + 1],
+                TILE >> depth_step + 1,
+                north_pos,
+                east_pos,
+                north_count,
+                east_count,
+            )
         )
-        own_field = crop_margin(grown, margin_now, 0)
-        coarse_normal = normalize(crop_margin(coarse, margin_next, 1))
+    level_field = crop_margin(levels[3], MARGINS[3], 0)
+    stacked = lax.all_gather(level_field[None], ("east", "north"), axis=0, tiled=True)
+    for depth_step in range(3):
+        own_field = crop_margin(levels[depth_step], MARGINS[depth_step], 0)
+        coarse_normal = normalize(crop_margin(levels[depth_step + 1], MARGINS[depth_step + 1], 1))
         laplace_band = normalize(own_field) - expand_padded(coarse_normal)
         results.append(laplace_band.astype(jnp.bfloat16))
-        grown = coarse
-    level_field = crop_margin(grown, MARGINS[3], 0)
-    stacked = lax.all_gather(level_field[None], ("east", "north"), axis=0, tiled=True)
     chan_count, tall_size, wide_size = level_field.shape
     whole_field = stacked.reshape(east_count, north_count, chan_count, tall_size, wide_size)
     whole_field = whole_field.transpose(2, 1, 3, 0, 4).reshape(

time: 306 us -> 298 us (0.974)
  matrix products: 68.6 us -> 32.4 us
  other arithmetic: 39.6 us -> 65.1 us
  waiting for transfers between devices: 113 us -> 122 us
  starting transfers between devices: 26.4 us -> 20.1 us
    dot_general x16 -> x17, matrix products: 55.6 us -> 22.8 us  [the longest x16 19 us: split_einsum(): term = jnp.einsum(spec, *pair, preferred_element_type=jnp.float32)]
    another operation x1 -> x20, other arithmetic: 0.76 us -> 20.9 us
    all_to_all x0 -> x2, local copies, waits for them, and re-layouts: none -> 11.5 us  [body(): lax.all_to_all(send, ('east', 'north'), split_axis=0, concat_axis=0, tile...]
    convert_element_type x1 -> x0, local copies, waits for them, and re-layouts: 8.93 us -> none  [body(): weighted = window_photos.astype(jnp.float32) * gain_value[:, None, :, :]]
    gather x2 -> x0, local copies, waits for them, and re-layouts: 8.56 us -> none  [the longest x1 7.96 us: body(): photos[source]]
    convert_element_type x1 -> x5, other arithmetic: 0.01 us -> 7.16 us  [the longest x3 5.24 us: body(): results.append(laplace_band.astype(jnp.bfloat16))]
    select_n x3 -> x0, other arithmetic: 6.62 us -> none  [the longest x1 5.93 us: body(): jnp.where(filled[:, None, None], photos[source], jnp.zeros((), jnp.bfloat...]
    all_to_all x2 -> x1, starting transfers between devices: 13.4 us -> 7.43 us  [body(): lax.all_to_all(send, ('east', 'north'), split_axis=0, concat_axis=0, tile...]
  transfers between devices with their start and end apart: 7 -> 6, of which waited for: 4 -> 4; matrix products, arithmetic and copies ran while one was open for 16% -> 9% of each run, Pallas kernels for 0% -> 0%
where the time goes in v1:
time: 298 us; the launch traced here: 293 us
  waiting for transfers between devices  122 us (41%)
  other arithmetic  65.1 us (22%)
  local copies, waits for them, and re-layouts  38.7 us (13%)
  matrix products  32.4 us (11%)
  starting transfers between devices  20.1 us (7%)
  between operations  14.9 us (5%)
    all_to_all x1, waiting for transfers between devices, body(): lax.all_to_all(send, ('east', 'north'), split_axis=0, concat_axis=0, tile...  76.6 us
    all_gather x1, waiting for transfers between devices, body(): lax.all_gather(level_field[None], ('east', 'north'), axis=0, tiled=True)  32.3 us
    another operation x20, other arithmetic  20.9 us
    dot_general x16, matrix products, split_einsum(): term = jnp.einsum(spec, *pair, preferred_element_type=jnp.float32)  19 us
    concatenate x1, other arithmetic, padded_2(): block = jnp.concatenate([low, block, high], axis=dim)  12.6 us
    ppermute x2, waiting for transfers between devices, padded_2(): lax.ppermute(lax.slice_in_dim(block, 0, width, axis=dim), axis, backward)  11.5 us
    all_to_all x2, local copies, waits for them, and re-layouts, body(): lax.all_to_all(send, ('east', 'north'), split_axis=0, concat_axis=0, tile...  11.5 us
    ppermute x2, starting transfers between devices, padded_2(): lax.ppermute(lax.slice_in_dim(block, block.shape[dim] - width, None, axis...  10.1 us
  transfers between devices with their start and end apart: 6, of which 4 were waited for; matrix products, arithmetic and copies ran while one was open for 9% of the time, Pallas kernels for 0%

profile of v1, /device:TPU:0, one launch (start us, length us, event | category | flops | bytes accessed | tf_op | source)
XLA Modules:
  0.0 293.2 jit_solution(6342098060368201709)
XLA Ops:
  11.7 4.5 %copy.125 = bf16[4,8,4,16384]{3,1,2,0:T(8,128)(2,1)S(1)} copy(bf16[4,8,4,16384]{3,2,1,0:T(4,128)(2,1)} %bitcast.241) | data formatting | bytes 8388608
  16.2 3.8 %convolution_convert_fusion = bf16[32,65664]{1,0:T(8,128)(2,1)} fusion(bf16[32,5]{1,0:T(8,128)(2,1)S(1)} %copy.124, bf16[32,65536]{1,0:T(8,128)(2,1)S(1)} %bitcast.242, s32[32]{0:T(128)S(1)} %multiply_add_fusion), kind=kOutput, calls=%fused_computation | convolution fusion | flops 149189632 | bytes 8397248 | tf_op jit(solution)/shard_map/sp,pj->sj/dot_general | solution.py:132
  19.9 5.5 %all_to_all.8 = bf16[16,2,65664]{2,1,0:T(2,128)(2,1)} reshape(bf16[32,65664]{1,0:T(8,128)(2,1)} %convolution_convert_fusion) | data formatting | bytes 8404992 | tf_op jit(solution)/shard_map/all_to_all | solution.py:135
  25.4 7.4 %all-to-all-start = ((bf16[16,2,65664]{2,1,0:T(2,128)(2,1)}), bf16[16,2,65664]{2,1,0:T(2,128)(2,1)}, u32[]{:S(2)}, u32[]{:S(2)}) async-start(bf16[16,2,65664]{2,1,0:T(2,128)(2,1)} %all_to_all.8), calls=%async_computation | async-start | bytes 8404992 | tf_op jit(solution)/shard_map/all_to_all | solution.py:135
  34.1 76.6 %all-to-all-done = bf16[16,2,65664]{2,1,0:T(2,128)(2,1)} async-done(((bf16[16,2,65664]{2,1,0:T(2,128)(2,1)}), bf16[16,2,65664]{2,1,0:T(2,128)(2,1)}, u32[]{:S(2)}, u32[]{:S(2)}) %all-to-all-start) | async-done | bytes 4202528 | tf_op jit(solution)/shard_map/all_to_all | solution.py:135
  110.7 6.0 %all_to_all.10 = bf16[32,65664]{1,0:T(8,128)(2,1)} reshape(bf16[16,2,65664]{2,1,0:T(2,128)(2,1)} %all-to-all-done) | data formatting | bytes 8404992 | tf_op jit(solution)/shard_map/all_to_all | solution.py:135
  117.8 2.7 convert_bitcast_fusion
  120.5 1.5 copy.126
  123.8 8.5 %fusion.3 = f32[16,4,128,128]{3,0,2,1:T(8,128)S(1)} fusion(f32[32,4,128,128]{3,2,1,0:T(8,128)S(1)} %bitcast.139, f32[32,128,128]{2,0,1:T(8,128)S(1)} %multiply_multiply_fusion, s32[32]{0:T(128)S(1)} %fusion.291), kind=kOutput, calls=%fused_computation.22 | convolution fusion | flops 404750848 | bytes 14680192 | tf_op jit(solution)/shard_map/bk,kcrs->bcrs/dot_general | solution.py:157
  132.3 2.8 fusion.154
  135.1 2.7 fusion.163
  137.9 1.7 maximum_maximum_fusion.2
  140.7 2.4 copy.95
  143.1 8.8 %collective-permute-start = (f32[5,512,22]{1,2,0:T(8,128)}, f32[5,512,22]{1,2,0:T(8,128)}, u32[]{:S(2)}, u32[]{:S(2)}) collective-permute-start(f32[5,512,22]{1,2,0:T(8,128)} %copy.95), channel_id=1, source_target_pairs={{0,2},{2,4},{4,6},{6,8},{8,10},{10,12},{12,14},{1,3},{3,5},{5,7},{... | collective-permute-start | bytes 675848 | tf_op jit(solution)/shard_map/ppermute | solution.py:23
  151.9 2.4 copy.96
  156.2 1.5 collective-permute-done
  157.7 2.4 copy.97
  160.1 11.5 %collective-permute-done.1 = f32[5,512,22]{1,2,0:T(8,128)} collective-permute-done((f32[5,512,22]{1,2,0:T(8,128)}, f32[5,512,22]{1,2,0:T(8,128)}, u32[]{:S(2)}, u32[]{:S(2)}) %collective-permute-start.1) | collective-permute-done | bytes 225312 | tf_op jit(solution)/shard_map/ppermute | solution.py:26
  171.6 2.4 copy.98
  174.1 12.6 %pad_maximum_fusion.1 = f32[5,512,556]{2,1,0:T(8,128)S(1)} fusion(f32[5,512,22]{2,1,0:T(8,128)} %copy.98, f32[5,128,128]{2,1,0:T(8,128)} %bitcast.231, f32[5,128,128]{2,1,0:T(8,128)} %bitcast.237, f32[5,128,128]{2,1,0:T(8,128)} %bitcast.225, f32[5,128,128]{2,1,0:T(8,128)} %bitcast.219, f32[5,128,128]{2,1,0:T(8,128)} %bitcast.213, ...), kind=kLoop, calls=%fused_computation.45 | loop fusion | flops 24197120 | bytes 11386880 | tf_op jit(solution)/shard_map/concatenate | solution.py:27
  189.5 3.2 %maximum_maximum_fusion = f32[5,512,512]{2,1,0:T(8,128)} fusion(f32[5,128,128]{2,1,0:T(8,128)S(1)} %bitcast.232, f32[5,128,128]{2,1,0:T(8,128)S(1)} %bitcast.238, f32[5,128,128]{2,1,0:T(8,128)S(1)} %bitcast.226, f32[5,128,128]{2,1,0:T(8,128)S(1)} %bitcast.220, f32[5,128,128]{2,1,0:T(8,128)S(1)} %bitcast.214, f32[5,128,128]{2,1,0:T(8,128)S(1)} %bitcast.208, ...), kind=kLoop, calls=%fused_computation.47 | loop fusion | flops 19660800 | bytes 10485760 | tf_op jit(solution)/shard_map/concatenate | solution.py:181
  194.8 12.2 %fusion.1 = (bf16[5,556,556]{2,1,0:T(8,128)(2,1)S(1)}, f32[5,556,556]{2,1,0:T(8,128)S(1)}) fusion(f32[5,22,556]{2,1,0:T(8,128)S(1)} %collective-permute-done.3, f32[5,512,22]{2,1,0:T(8,128)S(1)} %copy-done.13, f32[5,128,128]{2,1,0:T(8,128)S(1)} %bitcast.234, f32[5,128,128]{2,1,0:T(8,128)S(1)} %bitcast.240, f32[5,128,128]{2,1,0:T(8,128)S(1)} %bitcast.228, ...), kind=kLoop, calls=%fused_computation.18 | loop fusion | flops 35550640 | bytes 15456800 | tf_op jit(solution)/shard_map/convert.32
  208.2 3.7 %fusion.26 = f32[10,276,556]{2,1,0:T(8,128)S(1)} fusion(bf16[5,556,556]{2,1,0:T(8,128)(2,1)S(1)} %fusion.4, bf16[5,556,556]{2,1,0:T(8,128)(2,1)S(1)} %get-tuple-element.15, s32[276]{0:T(512)S(1)} %iota_multiply_fusion.1), kind=kOutput, calls=%fused_computation.70 | convolution fusion | flops 1711977344 | bytes 12322064 | tf_op jit(solution)/shard_map/ih,chw->ciw/dot_general | solution.py:45
  212.8 2.6 fusion.20
  228.3 1.8 convolution_bitcast_fusion
  230.7 2.9 fusion.36
  233.6 3.2 %fusion.17 = bf16[4,512,512]{2,1,0:T(8,128)(2,1)} fusion(f32[8,512,512]{2,1,0:T(8,128)S(1)} %fusion.36, f32[5,512,512]{2,1,0:T(8,128)S(1)} %bitcast.144, f32[512,512]{1,0:T(8,128)S(1)} %copy-done.16), kind=kLoop, calls=%fused_computation.56 | loop fusion | flops 4194304 | bytes 15728640 | tf_op jit(solution)/shard_map/convert_element_type | solution.py:205
  236.8 32.3 %all-gather.3.cloned.1.call-done = f32[80,64,64]{2,1,0:T(8,128)} async-done(((f32[5,64,64]{2,1,0:T(8,128)}), f32[80,64,64]{2,1,0:T(8,128)}) %all-gather.3.cloned.1.call-update) | async-done | bytes 1310736 | tf_op jit(solution)/shard_map/all_gather | solution.py:200
  269.2 3.4 %copy.130 = f32[8,2,5,64,64]{4,0,3,1,2:T(8,128)S(1)} copy(f32[8,2,5,64,64]{4,3,2,1,0:T(8,128)} %bitcast.243) | data formatting | bytes 2621440 | tf_op jit(solution)/shard_map/reshape | solution.py:207
  272.5 1.8 reshape.350
  274.4 1.5 slice.413
  282.9 2.0 fusion.118
  (131 shorter events, 39.8 us)
Async XLA Ops:
  25.4 85.3 %all-to-all-start = ((bf16[16,2,65664]{2,1,0:T(2,128)(2,1)}), bf16[16,2,65664]{2,1,0:T(2,128)(2,1)}, u32[]{:S(2)}, u32[]{:S(2)}) async-start(bf16[16,2,65664]{2,1,0:T(2,128)(2,1)} %all_to_all.8), calls=%async_computation | async-start | bytes 8404992 | tf_op jit(solution)/shard_map/all_to_all | solution.py:135
  32.9 236.3 %all-gather.3.cloned.1.call-start = ((), (), s32[]{:S(2)}) async-start(), calls=%async_computation.1 | async-start | bytes 2785280 | tf_op jit(solution)/shard_map/all_gather | solution.py:200
  137.8 1.7 copy-start
  137.8 1.7 copy-start.2
  137.8 1.7 copy-start.4
  137.8 1.7 copy-start.6
  137.9 1.7 copy-start.8
  137.9 1.7 copy-start.10
  143.1 14.5 %collective-permute-start = (f32[5,512,22]{1,2,0:T(8,128)}, f32[5,512,22]{1,2,0:T(8,128)}, u32[]{:S(2)}, u32[]{:S(2)}) collective-permute-start(f32[5,512,22]{1,2,0:T(8,128)} %copy.95), channel_id=1, source_target_pairs={{0,2},{2,4},{4,6},{6,8},{8,10},{10,12},{12,14},{1,3},{3,5},{5,7},{... | collective-permute-start | bytes 675848 | tf_op jit(solution)/shard_map/ppermute | solution.py:23
  154.3 17.3 %collective-permute-start.1 = (f32[5,512,22]{1,2,0:T(8,128)}, f32[5,512,22]{1,2,0:T(8,128)}, u32[]{:S(2)}, u32[]{:S(2)}) collective-permute-start(f32[5,512,22]{1,2,0:T(8,128)} %copy.96), channel_id=1, source_target_pairs={{2,0},{4,2},{6,4},{8,6},{10,8},{12,10},{14,12},{3,1},{5,3},{7,5},{... | collective-permute-start | bytes 675848 | tf_op jit(solution)/shard_map/ppermute | solution.py:26
  174.1 15.4 %copy-start.1 = (f32[1,5,128,128]{3,0,2,1:T(1,128)S(1)}, f32[1,5,128,128]{3,0,2,1:T(1,128)}, u32[]{:S(2)}) copy-start(f32[1,5,128,128]{3,0,2,1:T(1,128)} %copy-done) | copy-start | bytes 983044
  174.1 15.4 %copy-start.3 = (f32[1,5,128,128]{3,0,2,1:T(1,128)S(1)}, f32[1,5,128,128]{3,0,2,1:T(1,128)}, u32[]{:S(2)}) copy-start(f32[1,5,128,128]{3,0,2,1:T(1,128)} %copy-done.2) | copy-start | bytes 983044
  174.1 15.4 %copy-start.5 = (f32[1,5,128,128]{3,0,2,1:T(1,128)S(1)}, f32[1,5,128,128]{3,0,2,1:T(1,128)}, u32[]{:S(2)}) copy-start(f32[1,5,128,128]{3,0,2,1:T(1,128)} %copy-done.4) | copy-start | bytes 983044
  174.1 15.4 %copy-start.7 = (f32[1,5,128,128]{3,0,2,1:T(1,128)S(1)}, f32[1,5,128,128]{3,0,2,1:T(1,128)}, u32[]{:S(2)}) copy-start(f32[1,5,128,128]{3,0,2,1:T(1,128)} %copy-done.6) | copy-start | bytes 983044
  174.1 15.4 %copy-start.9 = (f32[1,5,128,128]{3,0,2,1:T(1,128)S(1)}, f32[1,5,128,128]{3,0,2,1:T(1,128)}, u32[]{:S(2)}) copy-start(f32[1,5,128,128]{3,0,2,1:T(1,128)} %copy-done.8) | copy-start | bytes 983044
  174.1 15.4 %copy-start.11 = (f32[1,5,128,128]{3,0,2,1:T(1,128)S(1)}, f32[1,5,128,128]{3,0,2,1:T(1,128)}, u32[]{:S(2)}) copy-start(f32[1,5,128,128]{3,0,2,1:T(1,128)} %copy-done.10) | copy-start | bytes 983044
  186.8 7.1 %collective-permute-start.2 = (f32[5,22,556]{2,1,0:T(8,128)S(1)}, f32[5,22,556]{2,1,0:T(8,128)S(1)}, u32[]{:S(2)}, u32[]{:S(2)}) collective-permute-start(f32[5,22,556]{2,1,0:T(8,128)S(1)} %get-tuple-element.19), channel_id=1, source_target_pairs={{0,1},{2,3},{4,5},{6,7},{8,9},{10,11},{12,13},{14,15},{16,17},{18,... | collective-permute-start | bytes 733928 | tf_op jit(solution)/shard_map/ppermute | solution.py:23
  188.1 5.8 %collective-permute-start.3 = (f32[5,22,556]{2,1,0:T(8,128)S(1)}, f32[5,22,556]{2,1,0:T(8,128)S(1)}, u32[]{:S(2)}, u32[]{:S(2)}) collective-permute-start(f32[5,22,556]{2,1,0:T(8,128)S(1)} %get-tuple-element.20), channel_id=1, source_target_pairs={{1,0},{3,2},{5,4},{7,6},{9,8},{11,10},{13,12},{15,14},{17,16},{19,... | collective-permute-start | bytes 733928 | tf_op jit(solution)/shard_map/ppermute | solution.py:26
  192.7 1.7 copy-start.12
  192.7 2.1 copy-start.13
  212.8 2.6 copy-start.17
  224.1 1.6 copy-start.18
  230.1 3.6 %slice-start = ((s8[5242880]{0:T(1024)(128)(4,1)}), s8[4194304]{0:T(1024)(128)(4,1)S(1)}, s32[]{:S(2)}) async-start(s8[5242880]{0:T(1024)(128)(4,1)} %bitcast.143), calls=%async_computation.2 | async-start | bytes 8388608
  230.7 2.9 slice-start.1
  230.7 2.9 copy-start.16
  274.4 2.3 copy-start.15
  274.4 3.0 %copy-start.19 = (s32[64]{0:T(128)S(1)}, s32[64]{0:T(128)}, u32[]{:S(2)}) copy-start(s32[64]{0:T(128)} %iota_multiply_fusion.5) | copy-start | bytes 772
  278.8 2.4 copy-start.14
Sparse Core Ops, SparseCore 0:
  222.6 46.4 all-gather.2

commit v2 on v1

--- a/solution.py
+++ b/solution.py
@@ -90,6 +90,50 @@
     col_keep = (col_global >= 0) & (col_global < east_count * tile_side)
     keep_table = (row_keep[:, None] & col_keep[None, :]).astype(jnp.float32)
     return grid_field * keep_table[None, :, :]
+
+
+def add_borders(field):
+    for axis, dim in (("east", 2), ("north", 1)):
+        count = lax.axis_size(axis)
+        forward = [(i, i + 1) for i in range(count - 1)]
+        backward = [(target, source) for source, target in forward]
+        size = field.shape[dim]
+        from_low = lax.ppermute(lax.slice_in_dim(field, size - 3, size, axis=dim), axis, forward)
+        from_high = lax.ppermute(lax.slice_in_dim(field, 0, 3, axis=dim), axis, backward)
+        pad_low = [(0, 0)] * 3
+        pad_high = [(0, 0)] * 3
+        pad_low[dim] = (1, size - 4)
+        pad_high[dim] = (size - 4, 1)
+        field = field + jnp.pad(from_low, pad_low) + jnp.pad(from_high, pad_high)
+    return crop_margin(field, 2, 1)
+
+
+def overlap_add(stacked, east_count, north_count):
+    chan_count, tall_span, wide_span = stacked.shape[1:]
+    tiles = stacked.reshape(east_count, north_count, chan_count, tall_span, wide_span)
+    for tile_axis, dim in ((0, 4), (1, 3)):
+        span = tiles.shape[dim]
+        core = lax.slice_in_dim(tiles, 2, span - 2, axis=dim)
+        low_spill = lax.slice_in_dim(tiles, 0, 2, axis=dim)
+        high_spill = lax.slice_in_dim(tiles, span - 2, span, axis=dim)
+        count = tiles.shape[tile_axis]
+        zero = jnp.zeros_like(lax.slice_in_dim(low_spill, 0, 1, axis=tile_axis))
+        into_last = jnp.concatenate(
+            [lax.slice_in_dim(low_spill, 1, count, axis=tile_axis), zero], axis=tile_axis
+        )
+        into_first = jnp.concatenate(
+            [zero, lax.slice_in_dim(high_spill, 0, count - 1, axis=tile_axis)], axis=tile_axis
+        )
+        inner = span - 4
+        pad_first = [(0, 0)] * 5
+        pad_last = [(0, 0)] * 5
+        pad_first[dim] = (0, inner - 2)
+        pad_last[dim] = (inner - 2, 0)
+        tiles = core + jnp.pad(into_first, pad_first) + jnp.pad(into_last, pad_last)
+    tall_size, wide_size = tiles.shape[3], tiles.shape[4]
+    return tiles.transpose(2, 1, 3, 0, 4).reshape(
+        chan_count, north_count * tall_size, east_count * wide_size
+    )
 
 
 def body(photos, footprint, placement, mask_rows, tile_scale):
@@ -182,13 +226,16 @@
     results = []
     east_pos = lax.axis_index("east")
     north_pos = lax.axis_index("north")
-    levels = [padded_2(canvas, (("east", 2), ("north", 1)), MARGINS[0])]
+    own_levels = [canvas]
+    spill_pad = 6
     for depth_step in range(3):
-        coarse = reduce_padded(levels[-1])
-        levels.append(
+        field = jnp.pad(
+            own_levels[-1], ((0, 0), (spill_pad, spill_pad), (spill_pad, spill_pad))
+        )
+        own_levels.append(
             mask_region(
-                coarse,
-                MARGINS[depth_step + 1],
+                reduce_padded(field),
+                2,
                 TILE >> depth_step + 1,
                 north_pos,
                 east_pos,
@@ -196,18 +243,16 @@
                 east_count,
             )
         )
-    level_field = crop_margin(levels[3], MARGINS[3], 0)
-    stacked = lax.all_gather(level_field[None], ("east", "north"), axis=0, tiled=True)
+        spill_pad = 4
+    stacked = lax.all_gather(own_levels[3][None], ("east", "north"), axis=0, tiled=True)
+    true_levels = [canvas] + [add_borders(own_levels[depth]) for depth in (1, 2, 3)]
     for depth_step in range(3):
-        own_field = crop_margin(levels[depth_step], MARGINS[depth_step], 0)
-        coarse_normal = normalize(crop_margin(levels[depth_step + 1], MARGINS[depth_step + 1], 1))
-        laplace_band = normalize(own_field) - expand_padded(coarse_normal)
+        own_field = true_levels[depth_step]
+        if depth_step:
+            own_field = crop_margin(own_field, 1, 0)
+        laplace_band = normalize(own_field) - expand_padded(normalize(true_levels[depth_step + 1]))
         results.append(laplace_band.astype(jnp.bfloat16))
-    chan_count, tall_size, wide_size = level_field.shape
-    whole_field = stacked.reshape(east_count, north_count, chan_count, tall_size, wide_size)
-    whole_field = whole_field.transpose(2, 1, 3, 0, 4).reshape(
-        chan_count, north_count * tall_size, east_count * wide_size
-    )
+    whole_field = overlap_add(stacked, east_count, north_count)
     top_field = reduce_padded(jnp.pad(whole_field, ((0, 0), (2, 2), (2, 2))))
     top_normal = normalize(top_field)
     band_three = (

time: 298 us -> 275 us (0.923)
  the two profiles are of different devices: /device:TPU:0 before, /device:TPU:15 now
where the time goes in v2:
time: 275 us; the launch traced here: 269 us
  waiting for transfers between devices  99.1 us (36%)
  local copies, waits for them, and re-layouts  42.1 us (15%)
  other arithmetic  41.9 us (15%)
  starting transfers between devices  38.9 us (14%)
  matrix products  32.1 us (12%)
  between operations  15.1 us (5%)
    all_to_all x1, waiting for transfers between devices, body(): lax.all_to_all(send, ('east', 'north'), split_axis=0, concat_axis=0, tile...  89.2 us
    dot_general x16, matrix products, split_einsum(): term = jnp.einsum(spec, *pair, preferred_element_type=jnp.float32)  18.6 us
    ppermute x6, starting transfers between devices, add_borders(): lax.ppermute(lax.slice_in_dim(field, 0, 3, axis=dim), axis, backward)  18.6 us
    ppermute x6, starting transfers between devices, add_borders(): lax.ppermute(lax.slice_in_dim(field, size - 3, size, axis=dim), axis, for...  13.7 us
    all_to_all x2, local copies, waits for them, and re-layouts, body(): lax.all_to_all(send, ('east', 'north'), split_axis=0, concat_axis=0, tile...  11.1 us
    unnamed x35, local copies, waits for them, and re-layouts  11 us
    ppermute x6, waiting for transfers between devices, add_borders(): lax.ppermute(lax.slice_in_dim(field, size - 3, size, axis=dim), axis, for...  9.87 us
    dot_general x1, matrix products, body(): jnp.einsum('bk,kcrs->bcrs', block_match, weighted, precision=lax.Precisio...  8.72 us
  transfers between devices with their start and end apart: 14, of which 2 were waited for; matrix products, arithmetic and copies ran while one was open for 12% of the time, Pallas kernels for 0%

profile of v2, /device:TPU:15, one launch (start us, length us, event | category | flops | bytes accessed | tf_op | source)
XLA Modules:
  0.0 269.3 jit_solution(6723057944259967308)
XLA Ops:
  11.7 4.5 %copy.139 = bf16[4,8,4,16384]{3,1,2,0:T(8,128)(2,1)S(1)} copy(bf16[4,8,4,16384]{3,2,1,0:T(4,128)(2,1)} %bitcast.143) | data formatting | bytes 8388608
  16.2 3.7 %convolution_convert_fusion = bf16[32,65664]{1,0:T(8,128)(2,1)} fusion(bf16[32,5]{1,0:T(8,128)(2,1)S(1)} %copy.138, bf16[32,65536]{1,0:T(8,128)(2,1)S(1)} %bitcast.144, s32[32]{0:T(128)S(1)} %multiply_add_fusion), kind=kOutput, calls=%fused_computation | convolution fusion | flops 149189632 | bytes 8397248 | tf_op jit(solution)/shard_map/sp,pj->sj/dot_general | solution.py:176
  19.9 5.5 %all_to_all.8 = bf16[16,2,65664]{2,1,0:T(2,128)(2,1)} reshape(bf16[32,65664]{1,0:T(8,128)(2,1)} %convolution_convert_fusion) | data formatting | bytes 8404992 | tf_op jit(solution)/shard_map/all_to_all | solution.py:179
  25.4 6.6 %all-to-all-start = ((bf16[16,2,65664]{2,1,0:T(2,128)(2,1)}), bf16[16,2,65664]{2,1,0:T(2,128)(2,1)}, u32[]{:S(2)}, u32[]{:S(2)}) async-start(bf16[16,2,65664]{2,1,0:T(2,128)(2,1)} %all_to_all.8), calls=%async_computation | async-start | bytes 8404992 | tf_op jit(solution)/shard_map/all_to_all | solution.py:179
  35.3 89.2 %all-to-all-done = bf16[16,2,65664]{2,1,0:T(2,128)(2,1)} async-done(((bf16[16,2,65664]{2,1,0:T(2,128)(2,1)}), bf16[16,2,65664]{2,1,0:T(2,128)(2,1)}, u32[]{:S(2)}, u32[]{:S(2)}) %all-to-all-start) | async-done | bytes 4202528 | tf_op jit(solution)/shard_map/all_to_all | solution.py:179
  124.6 5.6 %all_to_all.10 = bf16[32,65664]{1,0:T(8,128)(2,1)} reshape(bf16[16,2,65664]{2,1,0:T(2,128)(2,1)} %all-to-all-done) | data formatting | bytes 8404992 | tf_op jit(solution)/shard_map/all_to_all | solution.py:179
  131.3 2.7 %convert_bitcast_fusion = f32[4,8,512,128]{3,1,2,0:T(8,128)S(1)} fusion(bf16[32,65664]{1,0:T(8,128)(2,1)} %all_to_all.10), kind=kLoop, calls=%fused_computation.23 | loop fusion | flops 2097152 | bytes 12582912
  137.3 8.7 %fusion.3 = f32[16,4,128,128]{3,0,2,1:T(8,128)S(1)} fusion(f32[32,4,128,128]{3,2,1,0:T(8,128)S(1)} %bitcast.140, f32[32,128,128]{2,0,1:T(8,128)S(1)} %multiply_multiply_fusion, s32[32]{0:T(128)S(1)} %fusion.292), kind=kOutput, calls=%fused_computation.22 | convolution fusion | flops 404750848 | bytes 14680192 | tf_op jit(solution)/shard_map/bk,kcrs->bcrs/dot_general | solution.py:201
  146.0 2.7 %fusion.164 = (f32[1,5,128,128]{3,0,2,1:T(1,128)S(1)}, f32[1,5,128,128]{3,0,2,1:T(1,128)S(1)}, f32[1,5,128,128]{3,0,2,1:T(1,128)S(1)}, f32[1,5,128,128]{3,0,2,1:...) fusion(f32[16,4,128,128]{3,0,2,1:T(8,128)S(1)} %fusion.3, ...), kind=kLoop, calls=%fused_computation.242 | loop fusion | flops 573440 | bytes 7536640 | tf_op jit(solution)/shard_map/concatenate | solution.py:215
  148.7 2.7 %fusion.155 = (f32[1,5,128,128]{3,0,2,1:T(1,128)S(1)}, f32[1,5,128,128]{3,0,2,1:T(1,128)S(1)}, f32[1,5,128,128]{3,0,2,1:T(1,128)S(1)}, f32[1,5,128,128]{3,0,2,1:...) fusion(f32[16,4,128,128]{3,0,2,1:T(8,128)S(1)} %fusion.3, ...), kind=kLoop, calls=%fused_computation.233 | loop fusion | flops 737280 | bytes 8192000 | tf_op jit(solution)/shard_map/concatenate | solution.py:215
  152.1 2.5 fusion.1
  154.6 3.5 %fusion.28 = f32[10,260,524]{2,1,0:T(8,128)S(1)} fusion(bf16[5,524,524]{2,1,0:T(8,128)(2,1)S(1)} %get-tuple-element.14, bf16[5,524,524]{2,1,0:T(8,128)(2,1)S(1)} %get-tuple-element.13, s32[260]{0:T(512)S(1)} %iota_multiply_fusion.1), kind=kOutput, calls=%fused_computation.70 | convolution fusion | flops 1432720768 | bytes 10942160 | tf_op jit(solution)/shard_map/ih,chw->ciw/dot_general | solution.py:45
  159.0 2.5 fusion.20
  170.9 1.8 fusion.480
  172.6 2.8 %collective-permute-start.8 = (f32[5,68,3]{2,1,0:T(8,128)}, f32[5,68,3]{2,1,0:T(8,128)}, u32[]{:S(2)}, u32[]{:S(2)}) collective-permute-start(f32[5,68,3]{2,1,0:T(8,128)} %get-tuple-element.73), channel_id=1, source_target_pairs={{0,2},{2,4},{4,6},{6,8},{8,10},{10,12},{12,14},{1,3},{3,5},{5,7},{... | collective-permute-start | bytes 12248 | tf_op jit(solution)/shard_map/ppermute | solution.py:101
  175.4 2.5 collective-permute-start.9
  178.9 2.0 copy.102
  180.9 2.0 copy.104
  183.0 1.9 collective-permute-start.1
  184.9 4.3 %collective-permute-start = (f32[5,260,3]{1,2,0:T(4,128)}, f32[5,260,3]{1,2,0:T(4,128)}, u32[]{:S(2)}, u32[]{:S(2)}) collective-permute-start(f32[5,260,3]{1,2,0:T(4,128)} %copy.102), channel_id=1, source_target_pairs={{0,2},{2,4},{4,6},{6,8},{8,10},{10,12},{12,14},{1,3},{3,5},{5,7},{... | collective-permute-start | bytes 46808 | tf_op jit(solution)/shard_map/ppermute | solution.py:101
  189.1 2.8 %collective-permute-start.4 = (f32[5,132,3]{2,1,0:T(8,128)}, f32[5,132,3]{2,1,0:T(8,128)S(1)}, u32[]{:S(2)}, u32[]{:S(2)}) collective-permute-start(f32[5,132,3]{2,1,0:T(8,128)} %get-tuple-element.63), channel_id=1, source_target_pairs={{0,2},{2,4},{4,6},{6,8},{8,10},{10,12},{12,14},{1,3},{3,5},{5,7},{... | collective-permute-start | bytes 23768 | tf_op jit(solution)/shard_map/ppermute | solution.py:101
  192.0 2.5 collective-permute-start.5
  197.2 9.9 %collective-permute-done.4 = f32[5,132,3]{2,1,0:T(8,128)S(1)} collective-permute-done((f32[5,132,3]{2,1,0:T(8,128)}, f32[5,132,3]{2,1,0:T(8,128)S(1)}, u32[]{:S(2)}, u32[]{:S(2)}) %collective-permute-start.4) | collective-permute-done | bytes 7952 | tf_op jit(solution)/shard_map/ppermute | solution.py:101
  207.0 4.5 %collective-permute-start.11 = (f32[5,3,68]{2,1,0:T(4,128)S(1)}, f32[5,3,68]{2,1,0:T(4,128)S(1)}, u32[]{:S(2)}, u32[]{:S(2)}) collective-permute-start(f32[5,3,68]{2,1,0:T(4,128)S(1)} %get-tuple-element.72), channel_id=1, source_target_pairs={{1,0},{3,2},{5,4},{7,6},{9,8},{11,10},{13,12},{15,14},{17,16},{19,... | collective-permute-start | bytes 12248 | tf_op jit(solution)/shard_map/ppermute | solution.py:102
  214.1 4.2 %collective-permute-start.7 = (f32[5,3,132]{2,1,0:T(4,128)S(1)}, f32[5,3,132]{2,1,0:T(4,128)}, u32[]{:S(2)}, u32[]{:S(2)}) collective-permute-start(f32[5,3,132]{2,1,0:T(4,128)S(1)} %get-tuple-element.62), channel_id=1, source_target_pairs={{1,0},{3,2},{5,4},{7,6},{9,8},{11,10},{13,12},{15,14},{17,16},{19,... | collective-permute-start | bytes 23768 | tf_op jit(solution)/shard_map/ppermute | solution.py:102
  222.0 2.8 %pad_add_fusion.5 = f32[5,260,260]{2,1,0:T(8,128)S(1)} fusion(f32[5,260,3]{2,1,0:T(8,128)S(1)} %copy.105, f32[5,260,3]{2,1,0:T(8,128)S(1)} %copy.103, f32[260,260]{1,0:T(8,128)S(1)} %and_convert_fusion, f32[10,260,260]{2,1,0:T(8,128)} %copy-done.2), kind=kLoop, calls=%fused_computation.100 | loop fusion | flops 1352000 | bytes 4357600 | tf_op jit(solution)/shard_map/add | solution.py:107
  226.1 3.0 %collective-permute-start.3 = (f32[5,3,260]{2,1,0:T(4,128)S(1)}, f32[5,3,260]{2,1,0:T(4,128)S(1)}, u32[]{:S(2)}, u32[]{:S(2)}) collective-permute-start(f32[5,3,260]{2,1,0:T(4,128)S(1)} %get-tuple-element.44), channel_id=1, source_target_pairs={{1,0},{3,2},{5,4},{7,6},{9,8},{11,10},{13,12},{15,14},{17,16},{19,... | collective-permute-start | bytes 46808 | tf_op jit(solution)/shard_map/ppermute | solution.py:102
  234.8 1.8 convolution_bitcast_fusion
  237.3 2.9 %fusion.37 = f32[8,512,512]{2,1,0:T(8,128)S(1)} fusion(bf16[4,512,258]{1,2,0:T(8,128)(2,1)S(1)} %get-tuple-element.32, bf16[4,512,258]{1,2,0:T(8,128)(2,1)S(1)} %get-tuple-element.31, s32[258]{0:T(512)S(1)} %iota_multiply_fusion), kind=kOutput, calls=%fused_computation.85 | convolution fusion | flops 1085300736 | bytes 10503176 | tf_op jit(solution)/shard_map/ciw,jw->cij/dot_general | solution.py:45
  240.2 3.2 %fusion.17 = bf16[4,512,512]{2,1,0:T(8,128)(2,1)} fusion(f32[8,512,512]{2,1,0:T(8,128)S(1)} %fusion.37, f32[5,512,512]{2,1,0:T(8,128)S(1)} %bitcast.139, f32[512,512]{1,0:T(8,128)S(1)} %fusion.76), kind=kLoop, calls=%fused_computation.54 | loop fusion | flops 4194304 | bytes 15728640 | tf_op jit(solution)/shard_map/convert_element_type | solution.py:254
  243.4 2.8 %slice.488 = f32[8,2,5,68,64]{4,3,2,1,0:T(8,128)S(1)} slice(f32[8,2,5,68,68]{4,3,2,1,0:T(8,128)} %bitcast.141), slice={[0:8], [0:2], [0:5], [0:68], [2:66]} | slice | bytes 2785280 | tf_op jit(solution)/shard_map/slice | solution.py:116
  254.1 2.0 slice.391
  (146 shorter events, 54.1 us)
Async XLA Ops:
  25.4 99.2 %all-to-all-start = ((bf16[16,2,65664]{2,1,0:T(2,128)(2,1)}), bf16[16,2,65664]{2,1,0:T(2,128)(2,1)}, u32[]{:S(2)}, u32[]{:S(2)}) async-start(bf16[16,2,65664]{2,1,0:T(2,128)(2,1)} %all_to_all.8), calls=%async_computation | async-start | bytes 8404992 | tf_op jit(solution)/shard_map/all_to_all | solution.py:179
  31.9 211.5 %all-gather.3.cloned.1.call-start = ((), (), s32[]{:S(2)}) async-start(), calls=%async_computation.1 | async-start | bytes 3133440 | tf_op jit(solution)/shard_map/all_gather | solution.py:247
  33.0 132.4 %copy-start.9 = (s32[132]{0:T(256)}, s32[132]{0:T(256)S(1)}, u32[]{:S(2)}) copy-start(s32[132]{0:T(256)S(1)} %iota_multiply_fusion.4) | copy-start | bytes 1588
  152.0 2.7 copy-start
  161.4 2.0 copy-start.2
  166.5 0.7 copy-start.10
  166.5 1.5 copy-start.6
  167.1 1.3 copy-start.12
  168.1 2.0 copy-start.7
  169.4 0.7 copy-start.5
  172.6 19.3 %collective-permute-start.8 = (f32[5,68,3]{2,1,0:T(8,128)}, f32[5,68,3]{2,1,0:T(8,128)}, u32[]{:S(2)}, u32[]{:S(2)}) collective-permute-start(f32[5,68,3]{2,1,0:T(8,128)} %get-tuple-element.73), channel_id=1, source_target_pairs={{0,2},{2,4},{4,6},{6,8},{8,10},{10,12},{12,14},{1,3},{3,5},{5,7},{... | collective-permute-start | bytes 12248 | tf_op jit(solution)/shard_map/ppermute | solution.py:101
  175.4 19.0 %collective-permute-start.9 = (f32[5,68,3]{2,1,0:T(8,128)}, f32[5,68,3]{2,1,0:T(8,128)}, u32[]{:S(2)}, u32[]{:S(2)}) collective-permute-start(f32[5,68,3]{2,1,0:T(8,128)} %get-tuple-element.74), channel_id=1, source_target_pairs={{2,0},{4,2},{6,4},{8,6},{10,8},{12,10},{14,12},{3,1},{5,3},{7,5},{... | collective-permute-start | bytes 12248 | tf_op jit(solution)/shard_map/ppermute | solution.py:102
  183.0 38.0 %collective-permute-start.1 = (f32[5,260,3]{1,2,0:T(4,128)}, f32[5,260,3]{1,2,0:T(4,128)}, u32[]{:S(2)}, u32[]{:S(2)}) collective-permute-start(f32[5,260,3]{1,2,0:T(4,128)} %copy.104), channel_id=1, source_target_pairs={{2,0},{4,2},{6,4},{8,6},{10,8},{12,10},{14,12},{3,1},{5,3},{7,5},{... | collective-permute-start | bytes 46808 | tf_op jit(solution)/shard_map/ppermute | solution.py:102
  184.9 35.1 %collective-permute-start = (f32[5,260,3]{1,2,0:T(4,128)}, f32[5,260,3]{1,2,0:T(4,128)}, u32[]{:S(2)}, u32[]{:S(2)}) collective-permute-start(f32[5,260,3]{1,2,0:T(4,128)} %copy.102), channel_id=1, source_target_pairs={{0,2},{2,4},{4,6},{6,8},{8,10},{10,12},{12,14},{1,3},{3,5},{5,7},{... | collective-permute-start | bytes 46808 | tf_op jit(solution)/shard_map/ppermute | solution.py:101
  189.1 17.9 %collective-permute-start.4 = (f32[5,132,3]{2,1,0:T(8,128)}, f32[5,132,3]{2,1,0:T(8,128)S(1)}, u32[]{:S(2)}, u32[]{:S(2)}) collective-permute-start(f32[5,132,3]{2,1,0:T(8,128)} %get-tuple-element.63), channel_id=1, source_target_pairs={{0,2},{2,4},{4,6},{6,8},{8,10},{10,12},{12,14},{1,3},{3,5},{5,7},{... | collective-permute-start | bytes 23768 | tf_op jit(solution)/shard_map/ppermute | solution.py:101
  192.0 19.6 %collective-permute-start.5 = (f32[5,132,3]{2,1,0:T(8,128)}, f32[5,132,3]{2,1,0:T(8,128)S(1)}, u32[]{:S(2)}, u32[]{:S(2)}) collective-permute-start(f32[5,132,3]{2,1,0:T(8,128)} %get-tuple-element.64), channel_id=1, source_target_pairs={{2,0},{4,2},{6,4},{8,6},{10,8},{12,10},{14,12},{3,1},{5,3},{7,5},{... | collective-permute-start | bytes 23768 | tf_op jit(solution)/shard_map/ppermute | solution.py:102
  195.9 18.2 %collective-permute-start.10 = (f32[5,3,68]{2,1,0:T(4,128)S(1)}, f32[5,3,68]{2,1,0:T(4,128)S(1)}, u32[]{:S(2)}, u32[]{:S(2)}) collective-permute-start(f32[5,3,68]{2,1,0:T(4,128)S(1)} %get-tuple-element.71), channel_id=1, source_target_pairs={{0,1},{2,3},{4,5},{6,7},{8,9},{10,11},{12,13},{14,15},{16,17},{18,... | collective-permute-start | bytes 12248 | tf_op jit(solution)/shard_map/ppermute | solution.py:101
  207.0 11.2 %collective-permute-start.11 = (f32[5,3,68]{2,1,0:T(4,128)S(1)}, f32[5,3,68]{2,1,0:T(4,128)S(1)}, u32[]{:S(2)}, u32[]{:S(2)}) collective-permute-start(f32[5,3,68]{2,1,0:T(4,128)S(1)} %get-tuple-element.72), channel_id=1, source_target_pairs={{1,0},{3,2},{5,4},{7,6},{9,8},{11,10},{13,12},{15,14},{17,16},{19,... | collective-permute-start | bytes 12248 | tf_op jit(solution)/shard_map/ppermute | solution.py:102
  212.8 16.4 %collective-permute-start.6 = (f32[5,3,132]{2,1,0:T(4,128)S(1)}, f32[5,3,132]{2,1,0:T(4,128)}, u32[]{:S(2)}, u32[]{:S(2)}) collective-permute-start(f32[5,3,132]{2,1,0:T(4,128)S(1)} %get-tuple-element.61), channel_id=1, source_target_pairs={{0,1},{2,3},{4,5},{6,7},{8,9},{10,11},{12,13},{14,15},{16,17},{18,... | collective-permute-start | bytes 23768 | tf_op jit(solution)/shard_map/ppermute | solution.py:101
  214.1 15.1 %collective-permute-start.7 = (f32[5,3,132]{2,1,0:T(4,128)S(1)}, f32[5,3,132]{2,1,0:T(4,128)}, u32[]{:S(2)}, u32[]{:S(2)}) collective-permute-start(f32[5,3,132]{2,1,0:T(4,128)S(1)} %get-tuple-element.62), channel_id=1, source_target_pairs={{1,0},{3,2},{5,4},{7,6},{9,8},{11,10},{13,12},{15,14},{17,16},{19,... | collective-permute-start | bytes 23768 | tf_op jit(solution)/shard_map/ppermute | solution.py:102
  224.8 7.7 %collective-permute-start.2 = (f32[5,3,260]{2,1,0:T(4,128)S(1)}, f32[5,3,260]{2,1,0:T(4,128)S(1)}, u32[]{:S(2)}, u32[]{:S(2)}) collective-permute-start(f32[5,3,260]{2,1,0:T(4,128)S(1)} %get-tuple-element.43), channel_id=1, source_target_pairs={{0,1},{2,3},{4,5},{6,7},{8,9},{10,11},{12,13},{14,15},{16,17},{18,... | collective-permute-start | bytes 46808 | tf_op jit(solution)/shard_map/ppermute | solution.py:101
  226.1 6.4 %collective-permute-start.3 = (f32[5,3,260]{2,1,0:T(4,128)S(1)}, f32[5,3,260]{2,1,0:T(4,128)S(1)}, u32[]{:S(2)}, u32[]{:S(2)}) collective-permute-start(f32[5,3,260]{2,1,0:T(4,128)S(1)} %get-tuple-element.44), channel_id=1, source_target_pairs={{1,0},{3,2},{5,4},{7,6},{9,8},{11,10},{13,12},{15,14},{17,16},{19,... | collective-permute-start | bytes 46808 | tf_op jit(solution)/shard_map/ppermute | solution.py:102
  230.4 1.3 copy-start.4
  236.6 3.6 %slice-start = ((s8[5242880]{0:T(1024)(128)(4,1)}), s8[4194304]{0:T(1024)(128)(4,1)S(1)}, s32[]{:S(2)}) async-start(s8[5242880]{0:T(1024)(128)(4,1)} %bitcast.138), calls=%async_computation.2 | async-start | bytes 8388608
  237.3 2.9 %slice-start.1 = ((s8[5242880]{0:T(1024)(128)(4,1)}), s8[1048576]{0:T(1024)(128)(4,1)S(1)}, s32[]{:S(2)}) async-start(s8[5242880]{0:T(1024)(128)(4,1)} %bitcast.138), calls=%async_computation.3 | async-start | bytes 2097152
  243.4 2.8 %copy-start.1 = (f32[80,68,68]{2,1,0:T(8,128)S(1)}, f32[80,68,68]{2,1,0:T(8,128)}, u32[]{:S(2)}) copy-start(f32[80,68,68]{2,1,0:T(8,128)} %all-gather.3.cloned.1.call-done) | copy-start | bytes 4439044
  254.0 2.2 copy-start.3
  254.1 2.7 copy-start.11
  256.8 0.8 copy-start.8
Sparse Core Ops, SparseCore 0:
  179.0 46.5 all-gather.2

commit v3 on v2

--- a/solution.py
+++ b/solution.py
@@ -92,20 +92,31 @@
     return grid_field * keep_table[None, :, :]
 
 
-def add_borders(field):
+def add_borders(fields):
     for axis, dim in (("east", 2), ("north", 1)):
         count = lax.axis_size(axis)
         forward = [(i, i + 1) for i in range(count - 1)]
         backward = [(target, source) for source, target in forward]
-        size = field.shape[dim]
-        from_low = lax.ppermute(lax.slice_in_dim(field, size - 3, size, axis=dim), axis, forward)
-        from_high = lax.ppermute(lax.slice_in_dim(field, 0, 3, axis=dim), axis, backward)
-        pad_low = [(0, 0)] * 3
-        pad_high = [(0, 0)] * 3
-        pad_low[dim] = (1, size - 4)
-        pad_high[dim] = (size - 4, 1)
-        field = field + jnp.pad(from_low, pad_low) + jnp.pad(from_high, pad_high)
-    return crop_margin(field, 2, 1)
+        other = 3 - dim
+        lows = [lax.slice_in_dim(f, f.shape[dim] - 3, f.shape[dim], axis=dim) for f in fields]
+        highs = [lax.slice_in_dim(f, 0, 3, axis=dim) for f in fields]
+        from_low = lax.ppermute(jnp.concatenate(lows, axis=other), axis, forward)
+        from_high = lax.ppermute(jnp.concatenate(highs, axis=other), axis, backward)
+        updated = []
+        offset = 0
+        for f in fields:
+            size = f.shape[dim]
+            extent = f.shape[other]
+            low_part = lax.slice_in_dim(from_low, offset, offset + extent, axis=other)
+            high_part = lax.slice_in_dim(from_high, offset, offset + extent, axis=other)
+            offset += extent
+            pad_low = [(0, 0)] * 3
+            pad_high = [(0, 0)] * 3
+            pad_low[dim] = (1, size - 4)
+            pad_high[dim] = (size - 4, 1)
+            updated.append(f + jnp.pad(low_part, pad_low) + jnp.pad(high_part, pad_high))
+        fields = updated
+    return [crop_margin(f, 2, 1) for f in fields]
 
 
 def overlap_add(stacked, east_count, north_count):
@@ -245,7 +256,7 @@
         )
         spill_pad = 4
     stacked = lax.all_gather(own_levels[3][None], ("east", "north"), axis=0, tiled=True)
-    true_levels = [canvas] + [add_borders(own_levels[depth]) for depth in (1, 2, 3)]
+    true_levels = [canvas] + add_borders(own_levels[1:])
     for depth_step in range(3):
         own_field = true_levels[depth_step]
         if depth_step:

time: 275 us -> 272 us (0.989)
  the two profiles are of different devices: /device:TPU:15 before, /device:TPU:0 now
where the time goes in v3:
time: 272 us; the launch traced here: 267 us
  waiting for transfers between devices  121 us (44%)
  other arithmetic  39.3 us (14%)
  local copies, waits for them, and re-layouts  38.3 us (14%)
  matrix products  32.4 us (12%)
  starting transfers between devices  21.8 us (8%)
  between operations  15.1 us (6%)
    all_to_all x1, waiting for transfers between devices, body(): lax.all_to_all(send, ('east', 'north'), split_axis=0, concat_axis=0, tile...  77.2 us
    all_gather x1, waiting for transfers between devices, body(): lax.all_gather(own_levels[3][None], ('east', 'north'), axis=0, tiled=True)  41.6 us
    dot_general x16, matrix products, split_einsum(): term = jnp.einsum(spec, *pair, preferred_element_type=jnp.float32)  19 us
    unnamed x27, local copies, waits for them, and re-layouts  12.8 us
    ppermute x2, starting transfers between devices, add_borders(): from_low = lax.ppermute(jnp.concatenate(lows, axis=other), axis, forward)  11.8 us
    all_to_all x2, local copies, waits for them, and re-layouts, body(): lax.all_to_all(send, ('east', 'north'), split_axis=0, concat_axis=0, tile...  11.1 us
    another operation x17, other arithmetic  9.31 us
    dot_general x1, matrix products, body(): jnp.einsum('bk,kcrs->bcrs', block_match, weighted, precision=lax.Precisio...  8.72 us
  transfers between devices with their start and end apart: 6, of which 3 were waited for; matrix products, arithmetic and copies ran while one was open for 7% of the time, Pallas kernels for 0%

profile of v3, /device:TPU:0, one launch (start us, length us, event | category | flops | bytes accessed | tf_op | source)
XLA Modules:
  0.0 267.5 jit_solution(9788551309050346468)
XLA Ops:
  11.7 4.5 %copy.153 = bf16[4,8,4,16384]{3,1,2,0:T(8,128)(2,1)S(1)} copy(bf16[4,8,4,16384]{3,2,1,0:T(4,128)(2,1)} %bitcast.143) | data formatting | bytes 8388608
  16.2 3.7 %convolution_convert_fusion = bf16[32,65664]{1,0:T(8,128)(2,1)} fusion(bf16[32,5]{1,0:T(8,128)(2,1)S(1)} %copy.152, bf16[32,65536]{1,0:T(8,128)(2,1)S(1)} %bitcast.144, s32[32]{0:T(128)S(1)} %multiply_add_fusion), kind=kOutput, calls=%fused_computation | convolution fusion | flops 149189632 | bytes 8397248 | tf_op jit(solution)/shard_map/sp,pj->sj/dot_general | solution.py:187
  19.9 5.5 %all_to_all.8 = bf16[16,2,65664]{2,1,0:T(2,128)(2,1)} reshape(bf16[32,65664]{1,0:T(8,128)(2,1)} %convolution_convert_fusion) | data formatting | bytes 8404992 | tf_op jit(solution)/shard_map/all_to_all | solution.py:190
  25.4 7.4 %all-to-all-start = ((bf16[16,2,65664]{2,1,0:T(2,128)(2,1)}), bf16[16,2,65664]{2,1,0:T(2,128)(2,1)}, u32[]{:S(2)}, u32[]{:S(2)}) async-start(bf16[16,2,65664]{2,1,0:T(2,128)(2,1)} %all_to_all.8), calls=%async_computation | async-start | bytes 8404992 | tf_op jit(solution)/shard_map/all_to_all | solution.py:190
  33.4 77.2 %all-to-all-done = bf16[16,2,65664]{2,1,0:T(2,128)(2,1)} async-done(((bf16[16,2,65664]{2,1,0:T(2,128)(2,1)}), bf16[16,2,65664]{2,1,0:T(2,128)(2,1)}, u32[]{:S(2)}, u32[]{:S(2)}) %all-to-all-start) | async-done | bytes 4202528 | tf_op jit(solution)/shard_map/all_to_all | solution.py:190
  110.7 5.7 %all_to_all.10 = bf16[32,65664]{1,0:T(8,128)(2,1)} reshape(bf16[16,2,65664]{2,1,0:T(2,128)(2,1)} %all-to-all-done) | data formatting | bytes 8404992 | tf_op jit(solution)/shard_map/all_to_all | solution.py:190
  117.4 2.7 %convert_bitcast_fusion = f32[4,8,512,128]{3,1,2,0:T(8,128)S(1)} fusion(bf16[32,65664]{1,0:T(8,128)(2,1)} %all_to_all.10), kind=kLoop, calls=%fused_computation.23 | loop fusion | flops 2097152 | bytes 12582912
  121.9 1.5 copy.154
  123.4 8.7 %fusion.3 = f32[16,4,128,128]{3,0,2,1:T(8,128)S(1)} fusion(f32[32,4,128,128]{3,2,1,0:T(8,128)S(1)} %bitcast.140, f32[32,128,128]{2,0,1:T(8,128)S(1)} %multiply_multiply_fusion, s32[32]{0:T(128)S(1)} %fusion.292), kind=kOutput, calls=%fused_computation.22 | convolution fusion | flops 404750848 | bytes 14680192 | tf_op jit(solution)/shard_map/bk,kcrs->bcrs/dot_general | solution.py:212
  132.1 2.7 %fusion.164 = (f32[1,5,128,128]{3,0,2,1:T(1,128)S(1)}, f32[1,5,128,128]{3,0,2,1:T(1,128)S(1)}, f32[1,5,128,128]{3,0,2,1:T(1,128)S(1)}, f32[1,5,128,128]{3,0,2,1:...) fusion(f32[16,4,128,128]{3,0,2,1:T(8,128)S(1)} %fusion.3, ...), kind=kLoop, calls=%fused_computation.242 | loop fusion | flops 573440 | bytes 7536640 | tf_op jit(solution)/shard_map/concatenate | solution.py:226
  134.9 2.7 %fusion.155 = (f32[1,5,128,128]{3,0,2,1:T(1,128)S(1)}, f32[1,5,128,128]{3,0,2,1:T(1,128)S(1)}, f32[1,5,128,128]{3,0,2,1:T(1,128)S(1)}, f32[1,5,128,128]{3,0,2,1:...) fusion(f32[16,4,128,128]{3,0,2,1:T(8,128)S(1)} %fusion.3, ...), kind=kLoop, calls=%fused_computation.233 | loop fusion | flops 737280 | bytes 8192000 | tf_op jit(solution)/shard_map/concatenate | solution.py:226
  138.1 2.5 fusion.1
  140.7 3.5 %fusion.28 = f32[10,260,524]{2,1,0:T(8,128)S(1)} fusion(bf16[5,524,524]{2,1,0:T(8,128)(2,1)S(1)} %get-tuple-element.14, bf16[5,524,524]{2,1,0:T(8,128)(2,1)S(1)} %get-tuple-element.13, s32[260]{0:T(512)S(1)} %iota_multiply_fusion.1), kind=kOutput, calls=%fused_computation.70 | convolution fusion | flops 1432720768 | bytes 10942160 | tf_op jit(solution)/shard_map/ih,chw->ciw/dot_general | solution.py:45
  145.0 2.5 fusion.20
  147.7 1.7 copy-done.2
  154.8 1.4 copy.104
  157.1 1.6 convolution_bitcast_fusion.3
  159.6 1.3 collective-permute-start.1
  161.0 8.7 %collective-permute-start = (f32[5,460,3]{1,2,0:T(4,128)S(1)}, f32[5,460,3]{1,2,0:T(4,128)S(1)}, u32[]{:S(2)}, u32[]{:S(2)}) collective-permute-start(f32[5,460,3]{1,2,0:T(4,128)S(1)} %pad_maximum_fusion.1), channel_id=1, source_target_pairs={{0,2},{2,4},{4,6},{6,8},{8,10},{10,12},{12,14},{1,3},{3,5},{5,7},{... | collective-permute-start | bytes 82808 | tf_op jit(solution)/shard_map/ppermute | solution.py:103
  169.8 1.7 collective-permute-done
  175.3 2.9 %pad_add_fusion.5 = f32[5,260,260]{2,1,0:T(8,128)S(1)} fusion(f32[5,260,3]{2,1,0:T(8,128)} %copy.144, f32[5,260,3]{2,1,0:T(8,128)S(1)} %copy.143, f32[260,260]{1,0:T(8,128)S(1)} %and_convert_fusion, f32[10,260,260]{2,1,0:T(8,128)} %copy-done.2), kind=kLoop, calls=%fused_computation.100 | loop fusion | flops 1352000 | bytes 4357600 | tf_op jit(solution)/shard_map/add | solution.py:117
  179.7 3.0 %collective-permute-start.2 = (f32[5,3,460]{2,1,0:T(4,128)S(1)}, f32[5,3,460]{2,1,0:T(4,128)S(1)}, u32[]{:S(2)}, u32[]{:S(2)}) collective-permute-start(f32[5,3,460]{2,1,0:T(4,128)S(1)} %pad_maximum_fusion.3), channel_id=1, source_target_pairs={{0,1},{2,3},{4,5},{6,7},{8,9},{10,11},{12,13},{14,15},{16,17},{18,... | collective-permute-start | bytes 82808 | tf_op jit(solution)/shard_map/ppermute | solution.py:103
  182.8 1.3 fusion.76
  191.4 1.8 convolution_bitcast_fusion
  193.8 2.9 %fusion.37 = f32[8,512,512]{2,1,0:T(8,128)S(1)} fusion(bf16[4,512,258]{1,2,0:T(8,128)(2,1)S(1)} %get-tuple-element.32, bf16[4,512,258]{1,2,0:T(8,128)(2,1)S(1)} %get-tuple-element.31, s32[258]{0:T(512)S(1)} %iota_multiply_fusion), kind=kOutput, calls=%fused_computation.85 | convolution fusion | flops 1085300736 | bytes 10503176 | tf_op jit(solution)/shard_map/ciw,jw->cij/dot_general | solution.py:45
  196.7 3.2 %fusion.17 = bf16[4,512,512]{2,1,0:T(8,128)(2,1)} fusion(f32[8,512,512]{2,1,0:T(8,128)S(1)} %fusion.37, f32[5,512,512]{2,1,0:T(8,128)S(1)} %bitcast.139, f32[512,512]{1,0:T(8,128)S(1)} %fusion.76), kind=kLoop, calls=%fused_computation.54 | loop fusion | flops 4194304 | bytes 15728640 | tf_op jit(solution)/shard_map/convert_element_type | solution.py:265
  199.9 41.6 %all-gather.3.cloned.1.call-done = f32[80,68,68]{2,1,0:T(8,128)} async-done(((f32[5,68,68]{2,1,0:T(8,128)}), f32[80,68,68]{2,1,0:T(8,128)}) %all-gather.3.cloned.1.call-update) | async-done | bytes 1479696 | tf_op jit(solution)/shard_map/all_gather | solution.py:258
  241.6 2.8 %slice.548 = f32[8,2,5,68,64]{4,3,2,1,0:T(8,128)S(1)} slice(f32[8,2,5,68,68]{4,3,2,1,0:T(8,128)} %bitcast.141), slice={[0:8], [0:2], [0:5], [0:68], [2:66]} | slice | bytes 2785280 | tf_op jit(solution)/shard_map/slice | solution.py:127
  247.2 1.5 pad_add_fusion
  249.0 1.7 reshape.350
  250.7 1.5 slice.554
  252.3 2.0 slice.439
  (140 shorter events, 38.8 us)
Async XLA Ops:
  25.4 85.3 %all-to-all-start = ((bf16[16,2,65664]{2,1,0:T(2,128)(2,1)}), bf16[16,2,65664]{2,1,0:T(2,128)(2,1)}, u32[]{:S(2)}, u32[]{:S(2)}) async-start(bf16[16,2,65664]{2,1,0:T(2,128)(2,1)} %all_to_all.8), calls=%async_computation | async-start | bytes 8404992 | tf_op jit(solution)/shard_map/all_to_all | solution.py:190
  32.8 208.7 %all-gather.3.cloned.1.call-start = ((), (), s32[]{:S(2)}) async-start(), calls=%async_computation.1 | async-start | bytes 3133440 | tf_op jit(solution)/shard_map/all_gather | solution.py:258
  138.1 2.5 copy-start
  147.4 2.0 copy-start.2
  159.2 13.8 %copy-start.5 = (f32[5,68,68]{2,1,0:T(8,128)}, f32[5,68,68]{2,1,0:T(8,128)S(1)}, u32[]{:S(2)}) copy-start(f32[5,68,68]{2,1,0:T(8,128)S(1)} %fusion.206) | copy-start | bytes 277444
  159.6 12.1 %collective-permute-start.1 = (f32[5,460,3]{1,2,0:T(4,128)S(1)}, f32[5,460,3]{1,2,0:T(4,128)S(1)}, u32[]{:S(2)}, u32[]{:S(2)}) collective-permute-start(f32[5,460,3]{1,2,0:T(4,128)S(1)} %pad_maximum_fusion.2), channel_id=1, source_target_pairs={{2,0},{4,2},{6,4},{8,6},{10,8},{12,10},{14,12},{3,1},{5,3},{7,5},{... | collective-permute-start | bytes 82808 | tf_op jit(solution)/shard_map/ppermute | solution.py:104
  161.0 10.5 %collective-permute-start = (f32[5,460,3]{1,2,0:T(4,128)S(1)}, f32[5,460,3]{1,2,0:T(4,128)S(1)}, u32[]{:S(2)}, u32[]{:S(2)}) collective-permute-start(f32[5,460,3]{1,2,0:T(4,128)S(1)} %pad_maximum_fusion.1), channel_id=1, source_target_pairs={{0,2},{2,4},{4,6},{6,8},{8,10},{10,12},{12,14},{1,3},{3,5},{5,7},{... | collective-permute-start | bytes 82808 | tf_op jit(solution)/shard_map/ppermute | solution.py:103
  173.0 0.9 copy-start.4
  178.3 5.8 %collective-permute-start.3 = (f32[5,3,460]{2,1,0:T(4,128)S(1)}, f32[5,3,460]{2,1,0:T(4,128)S(1)}, u32[]{:S(2)}, u32[]{:S(2)}) collective-permute-start(f32[5,3,460]{2,1,0:T(4,128)S(1)} %pad_maximum_fusion.4), channel_id=1, source_target_pairs={{1,0},{3,2},{5,4},{7,6},{9,8},{11,10},{13,12},{15,14},{17,16},{19,... | collective-permute-start | bytes 82808 | tf_op jit(solution)/shard_map/ppermute | solution.py:104
  179.7 4.5 %collective-permute-start.2 = (f32[5,3,460]{2,1,0:T(4,128)S(1)}, f32[5,3,460]{2,1,0:T(4,128)S(1)}, u32[]{:S(2)}, u32[]{:S(2)}) collective-permute-start(f32[5,3,460]{2,1,0:T(4,128)S(1)} %pad_maximum_fusion.3), channel_id=1, source_target_pairs={{0,1},{2,3},{4,5},{6,7},{8,9},{10,11},{12,13},{14,15},{16,17},{18,... | collective-permute-start | bytes 82808 | tf_op jit(solution)/shard_map/ppermute | solution.py:103
  193.2 3.6 %slice-start = ((s8[5242880]{0:T(1024)(128)(4,1)}), s8[4194304]{0:T(1024)(128)(4,1)S(1)}, s32[]{:S(2)}) async-start(s8[5242880]{0:T(1024)(128)(4,1)} %bitcast.138), calls=%async_computation.2 | async-start | bytes 8388608
  193.8 2.9 %slice-start.1 = ((s8[5242880]{0:T(1024)(128)(4,1)}), s8[1048576]{0:T(1024)(128)(4,1)S(1)}, s32[]{:S(2)}) async-start(s8[5242880]{0:T(1024)(128)(4,1)} %bitcast.138), calls=%async_computation.3 | async-start | bytes 2097152
  241.6 2.8 %copy-start.1 = (f32[80,68,68]{2,1,0:T(8,128)S(1)}, f32[80,68,68]{2,1,0:T(8,128)}, u32[]{:S(2)}) copy-start(f32[80,68,68]{2,1,0:T(8,128)} %all-gather.3.cloned.1.call-done) | copy-start | bytes 4439044
  252.2 2.2 copy-start.3
Sparse Core Ops, SparseCore 0:
  184.2 57.2 all-gather.2

commit v4 on v3

--- a/solution.py
+++ b/solution.py
@@ -255,7 +255,14 @@
             )
         )
         spill_pad = 4
-    stacked = lax.all_gather(own_levels[3][None], ("east", "north"), axis=0, tiled=True)
+    patch = own_levels[3]
+    patch_size = patch.size
+    lane_rows = -(-patch_size // 128)
+    flat = jnp.pad(patch.reshape(patch_size), (0, lane_rows * 128 - patch_size))
+    gathered = lax.all_gather(flat.reshape(1, lane_rows, 128), ("east", "north"), axis=0, tiled=True)
+    stacked = gathered.reshape(gathered.shape[0], lane_rows * 128)[:, :patch_size].reshape(
+        (gathered.shape[0],) + patch.shape
+    )
     true_levels = [canvas] + add_borders(own_levels[1:])
     for depth_step in range(3):
         own_field = true_levels[depth_step]

time: 272 us -> 282 us (1.037)
  local copies, waits for them, and re-layouts: 38.3 us -> 51.2 us
  waiting for transfers between devices: 121 us -> 111 us
  other arithmetic: 39.3 us -> 45.5 us
    all_gather x1, waiting for transfers between devices: 41.6 us -> 35.2 us  [body(): lax.all_gather(flat.reshape(1, lane_rows, 128), ('east', 'north'), axis=0...]
    unnamed x27 -> x36, local copies, waits for them, and re-layouts: 12.8 us -> 17.3 us
    another operation x0 -> x1, local copies, waits for them, and re-layouts: none -> 3.26 us  [overlap_add(): stacked.reshape(east_count, north_count, chan_count, tall_span, wide_span)]
    transpose x0 -> x1, local copies, waits for them, and re-layouts: none -> 3.19 us  [overlap_add(): tiles.transpose(2, 1, 3, 0, 4)]
    add x6, other arithmetic: 4.69 us -> 7.83 us  [add_borders(): f + jnp.pad(low_part, pad_low) + jnp.pad(high_part, pad_high)]
  transfers between devices with their start and end apart: 6 -> 6, of which waited for: 3 -> 3; matrix products, arithmetic and copies ran while one was open for 7% -> 8% of each run, Pallas kernels for 0% -> 0%
where the time goes in v4:
time: 282 us; the launch traced here: 277 us
  waiting for transfers between devices  111 us (39%)
  local copies, waits for them, and re-layouts  51.2 us (18%)
  other arithmetic  45.5 us (16%)
  matrix products  32.5 us (12%)
  starting transfers between devices  21.8 us (8%)
  between operations  15.1 us (5%)
    all_to_all x1, waiting for transfers between devices, body(): lax.all_to_all(send, ('east', 'north'), split_axis=0, concat_axis=0, tile...  75.7 us
    all_gather x1, waiting for transfers between devices, body(): lax.all_gather(flat.reshape(1, lane_rows, 128), ('east', 'north'), axis=0...  35.2 us
    dot_general x16, matrix products, split_einsum(): term = jnp.einsum(spec, *pair, preferred_element_type=jnp.float32)  19 us
    unnamed x36, local copies, waits for them, and re-layouts  17.3 us
    ppermute x2, starting transfers between devices, add_borders(): from_low = lax.ppermute(jnp.concatenate(lows, axis=other), axis, forward)  11.7 us
    all_to_all x2, local copies, waits for them, and re-layouts, body(): lax.all_to_all(send, ('east', 'north'), split_axis=0, concat_axis=0, tile...  11.1 us
    another operation x17, other arithmetic  9.32 us
    dot_general x1, matrix products, body(): jnp.einsum('bk,kcrs->bcrs', block_match, weighted, precision=lax.Precisio...  8.72 us
  transfers between devices with their start and end apart: 6, of which 3 were waited for; matrix products, arithmetic and copies ran while one was open for 8% of the time, Pallas kernels for 0%

profile of v4, /device:TPU:0, one launch (start us, length us, event | category | flops | bytes accessed | tf_op | source)
XLA Modules:
  0.0 277.1 jit_solution(5867505510529443255)
XLA Ops:
  11.7 4.5 %copy.147 = bf16[4,8,4,16384]{3,1,2,0:T(8,128)(2,1)S(1)} copy(bf16[4,8,4,16384]{3,2,1,0:T(4,128)(2,1)} %bitcast.148) | data formatting | bytes 8388608
  16.2 3.8 %convolution_convert_fusion = bf16[32,65664]{1,0:T(8,128)(2,1)} fusion(bf16[32,5]{1,0:T(8,128)(2,1)S(1)} %copy.146, bf16[32,65536]{1,0:T(8,128)(2,1)S(1)} %bitcast.149, s32[32]{0:T(128)S(1)} %multiply_add_fusion), kind=kOutput, calls=%fused_computation | convolution fusion | flops 149189632 | bytes 8397248 | tf_op jit(solution)/shard_map/sp,pj->sj/dot_general | solution.py:187
  19.9 5.5 %all_to_all.8 = bf16[16,2,65664]{2,1,0:T(2,128)(2,1)} reshape(bf16[32,65664]{1,0:T(8,128)(2,1)} %convolution_convert_fusion) | data formatting | bytes 8404992 | tf_op jit(solution)/shard_map/all_to_all | solution.py:190
  25.4 7.4 %all-to-all-start = ((bf16[16,2,65664]{2,1,0:T(2,128)(2,1)}), bf16[16,2,65664]{2,1,0:T(2,128)(2,1)}, u32[]{:S(2)}, u32[]{:S(2)}) async-start(bf16[16,2,65664]{2,1,0:T(2,128)(2,1)} %all_to_all.8), calls=%async_computation | async-start | bytes 8404992 | tf_op jit(solution)/shard_map/all_to_all | solution.py:190
  35.0 75.7 %all-to-all-done = bf16[16,2,65664]{2,1,0:T(2,128)(2,1)} async-done(((bf16[16,2,65664]{2,1,0:T(2,128)(2,1)}), bf16[16,2,65664]{2,1,0:T(2,128)(2,1)}, u32[]{:S(2)}, u32[]{:S(2)}) %all-to-all-start) | async-done | bytes 4202528 | tf_op jit(solution)/shard_map/all_to_all | solution.py:190
  110.7 5.6 %all_to_all.10 = bf16[32,65664]{1,0:T(8,128)(2,1)} reshape(bf16[16,2,65664]{2,1,0:T(2,128)(2,1)} %all-to-all-done) | data formatting | bytes 8404992 | tf_op jit(solution)/shard_map/all_to_all | solution.py:190
  117.4 2.7 convert_bitcast_fusion
  121.9 1.5 copy.148
  123.4 8.7 %fusion.3 = f32[16,4,128,128]{3,0,2,1:T(8,128)S(1)} fusion(f32[32,4,128,128]{3,2,1,0:T(8,128)S(1)} %bitcast.146, f32[32,128,128]{2,0,1:T(8,128)S(1)} %multiply_multiply_fusion, s32[32]{0:T(128)S(1)} %fusion.292), kind=kOutput, calls=%fused_computation.22 | convolution fusion | flops 404750848 | bytes 14680192 | tf_op jit(solution)/shard_map/bk,kcrs->bcrs/dot_general | solution.py:212
  132.1 2.7 fusion.164
  134.9 2.7 fusion.155
  138.1 2.5 fusion.1
  140.7 3.5 %fusion.28 = f32[10,260,524]{2,1,0:T(8,128)S(1)} fusion(bf16[5,524,524]{2,1,0:T(8,128)(2,1)S(1)} %get-tuple-element.14, bf16[5,524,524]{2,1,0:T(8,128)(2,1)S(1)} %get-tuple-element.13, s32[260]{0:T(512)S(1)} %iota_multiply_fusion.1), kind=kOutput, calls=%fused_computation.72 | convolution fusion | flops 1432720768 | bytes 10942160 | tf_op jit(solution)/shard_map/ih,chw->ciw/dot_general | solution.py:45
  145.0 2.5 fusion.20
  147.7 1.7 copy-done.2
  157.9 1.6 convolution_bitcast_fusion.3
  163.1 8.7 %collective-permute-start = (f32[5,460,3]{1,2,0:T(4,128)}, f32[5,460,3]{1,2,0:T(4,128)S(1)}, u32[]{:S(2)}, u32[]{:S(2)}) collective-permute-start(f32[5,460,3]{1,2,0:T(4,128)} %pad_maximum_fusion.1), channel_id=1, source_target_pairs={{0,2},{2,4},{4,6},{6,8},{8,10},{10,12},{12,14},{1,3},{3,5},{5,7},{... | collective-permute-start | bytes 82808 | tf_op jit(solution)/shard_map/ppermute | solution.py:103
  171.8 1.3 fusion.76
  183.3 3.1 %pad_add_fusion.5 = f32[5,260,260]{2,1,0:T(8,128)S(1)} fusion(f32[5,260,3]{2,1,0:T(8,128)} %copy.141, f32[5,260,3]{2,1,0:T(8,128)} %copy.140, f32[260,260]{1,0:T(8,128)S(1)} %and_convert_fusion, f32[10,260,260]{2,1,0:T(8,128)} %copy-done.2), kind=kLoop, calls=%fused_computation.100 | loop fusion | flops 1352000 | bytes 4357600 | tf_op jit(solution)/shard_map/add | solution.py:117
  186.5 1.3 collective-permute-start.3
  187.9 3.0 %collective-permute-start.2 = (f32[5,3,460]{2,1,0:T(4,128)S(1)}, f32[5,3,460]{2,1,0:T(4,128)S(1)}, u32[]{:S(2)}, u32[]{:S(2)}) collective-permute-start(f32[5,3,460]{2,1,0:T(4,128)S(1)} %pad_maximum_fusion.3), channel_id=1, source_target_pairs={{0,1},{2,3},{4,5},{6,7},{8,9},{10,11},{12,13},{14,15},{16,17},{18,... | collective-permute-start | bytes 82808 | tf_op jit(solution)/shard_map/ppermute | solution.py:103
  199.9 1.8 convolution_bitcast_fusion
  202.4 2.9 %fusion.37 = f32[8,512,512]{2,1,0:T(8,128)S(1)} fusion(bf16[4,512,258]{1,2,0:T(8,128)(2,1)S(1)} %get-tuple-element.32, bf16[4,512,258]{1,2,0:T(8,128)(2,1)S(1)} %get-tuple-element.31, s32[258]{0:T(512)S(1)} %iota_multiply_fusion), kind=kOutput, calls=%fused_computation.85 | convolution fusion | flops 1085300736 | bytes 10503176 | tf_op jit(solution)/shard_map/ciw,jw->cij/dot_general | solution.py:45
  205.3 3.2 %fusion.17 = bf16[4,512,512]{2,1,0:T(8,128)(2,1)} fusion(f32[8,512,512]{2,1,0:T(8,128)S(1)} %fusion.37, f32[5,512,512]{2,1,0:T(8,128)S(1)} %bitcast.145, f32[512,512]{1,0:T(8,128)S(1)} %fusion.76), kind=kLoop, calls=%fused_computation.54 | loop fusion | flops 4194304 | bytes 15728640 | tf_op jit(solution)/shard_map/convert_element_type | solution.py:272
  208.5 35.2 %all-gather.2.cloned.1.call-done = f32[16,181,128]{2,1,0:T(8,128)} async-done(((f32[1,181,128]{2,1,0:T(8,128)}), f32[16,181,128]{2,1,0:T(8,128)}) %all-gather.2.cloned.1.call-update) | async-done | bytes 1482768 | tf_op jit(solution)/shard_map/all_gather | solution.py:262
  243.6 2.8 %copy.153 = f32[2,8,181,128]{3,1,2,0:T(8,128)} copy(f32[2,8,181,128]{3,2,1,0:T(8,128)} %bitcast.150) | data formatting | bytes 2965504
  246.5 3.3 %reshape_reshape.3 = f32[8,2,5,68,68]{4,3,2,1,0:T(8,128)S(1)} reshape(f32[16,23120]{1,0:T(8,128)} %bitcast.147) | data formatting | bytes 2959360 | tf_op jit(solution)/shard_map/reshape;reshape | solution.py:124
  250.6 1.6 pad_add_fusion
  252.7 3.2 %copy.118 = f32[5,2,64,8,64]{4,3,2,1,0:T(8,128)} copy(f32[5,2,64,8,64]{4,2,0,1,3:T(8,128)S(1)} %fusion.33) | data formatting | bytes 2621440 | tf_op jit(solution)/shard_map/transpose | solution.py:145
  257.0 2.0 reshape.358
  259.1 2.6 copy.116
  261.7 2.2 slice.443
  (155 shorter events, 51.1 us)
Async XLA Ops:
  25.4 85.3 %all-to-all-start = ((bf16[16,2,65664]{2,1,0:T(2,128)(2,1)}), bf16[16,2,65664]{2,1,0:T(2,128)(2,1)}, u32[]{:S(2)}, u32[]{:S(2)}) async-start(bf16[16,2,65664]{2,1,0:T(2,128)(2,1)} %all_to_all.8), calls=%async_computation | async-start | bytes 8404992 | tf_op jit(solution)/shard_map/all_to_all | solution.py:190
  32.8 210.8 %all-gather.2.cloned.1.call-start = ((), (), s32[]{:S(2)}) async-start(), calls=%async_computation.1 | async-start | bytes 1601536 | tf_op jit(solution)/shard_map/all_gather | solution.py:262
  34.9 117.7 %copy-start.4 = (f32[132,132]{1,0:T(8,128)}, f32[132,132]{1,0:T(8,128)S(1)}, u32[]{:S(2)}) copy-start(f32[132,132]{1,0:T(8,128)S(1)} %and_convert_fusion.1) | copy-start | bytes 209092
  138.1 2.5 copy-start
  147.4 2.0 copy-start.2
  161.1 13.7 %collective-permute-start.1 = (f32[5,460,3]{1,2,0:T(4,128)}, f32[5,460,3]{1,2,0:T(4,128)S(1)}, u32[]{:S(2)}, u32[]{:S(2)}) collective-permute-start(f32[5,460,3]{1,2,0:T(4,128)} %pad_maximum_fusion.2), channel_id=1, source_target_pairs={{2,0},{4,2},{6,4},{8,6},{10,8},{12,10},{14,12},{3,1},{5,3},{7,5},{... | collective-permute-start | bytes 82808 | tf_op jit(solution)/shard_map/ppermute | solution.py:104
  163.1 10.8 %collective-permute-start = (f32[5,460,3]{1,2,0:T(4,128)}, f32[5,460,3]{1,2,0:T(4,128)S(1)}, u32[]{:S(2)}, u32[]{:S(2)}) collective-permute-start(f32[5,460,3]{1,2,0:T(4,128)} %pad_maximum_fusion.1), channel_id=1, source_target_pairs={{0,2},{2,4},{4,6},{6,8},{8,10},{10,12},{12,14},{1,3},{3,5},{5,7},{... | collective-permute-start | bytes 82808 | tf_op jit(solution)/shard_map/ppermute | solution.py:103
  176.9 0.7 copy-start.6
  180.1 0.9 copy-start.3
  183.3 7.7 %copy-start.7 = (f32[23120]{0:T(1024)S(1)}, f32[23120]{0:T(1024)}, u32[]{:S(2)}) copy-start(f32[23120]{0:T(1024)} %reshape.355) | copy-start | bytes 277444
  186.5 5.1 %collective-permute-start.3 = (f32[5,3,460]{2,1,0:T(4,128)S(1)}, f32[5,3,460]{2,1,0:T(4,128)S(1)}, u32[]{:S(2)}, u32[]{:S(2)}) collective-permute-start(f32[5,3,460]{2,1,0:T(4,128)S(1)} %pad_maximum_fusion.4), channel_id=1, source_target_pairs={{1,0},{3,2},{5,4},{7,6},{9,8},{11,10},{13,12},{15,14},{17,16},{19,... | collective-permute-start | bytes 82808 | tf_op jit(solution)/shard_map/ppermute | solution.py:104
  187.9 3.9 %collective-permute-start.2 = (f32[5,3,460]{2,1,0:T(4,128)S(1)}, f32[5,3,460]{2,1,0:T(4,128)S(1)}, u32[]{:S(2)}, u32[]{:S(2)}) collective-permute-start(f32[5,3,460]{2,1,0:T(4,128)S(1)} %pad_maximum_fusion.3), channel_id=1, source_target_pairs={{0,1},{2,3},{4,5},{6,7},{8,9},{10,11},{12,13},{14,15},{16,17},{18,... | collective-permute-start | bytes 82808 | tf_op jit(solution)/shard_map/ppermute | solution.py:103
  194.9 0.6 copy-start.8
  201.7 3.6 %slice-start = ((s8[5242880]{0:T(1024)(128)(4,1)}), s8[4194304]{0:T(1024)(128)(4,1)S(1)}, s32[]{:S(2)}) async-start(s8[5242880]{0:T(1024)(128)(4,1)} %bitcast.144), calls=%async_computation.2 | async-start | bytes 8388608
  202.4 2.9 %slice-start.1 = ((s8[5242880]{0:T(1024)(128)(4,1)}), s8[1048576]{0:T(1024)(128)(4,1)S(1)}, s32[]{:S(2)}) async-start(s8[5242880]{0:T(1024)(128)(4,1)} %bitcast.144), calls=%async_computation.3 | async-start | bytes 2097152
  252.6 3.3 %copy-start.1 = (f32[5,2,64,8,64]{4,2,0,1,3:T(8,128)}, f32[5,2,64,8,64]{4,2,0,1,3:T(8,128)S(1)}, u32[]{:S(2)}) copy-start(f32[5,2,64,8,64]{4,2,0,1,3:T(8,128)S(1)} %fusion.33) | copy-start | bytes 3932164
  256.2 2.9 %slice-start.2 = ((f32[5,2,64,8,64]{4,2,0,1,3:T(8,128)}), f32[4,2,64,8,64]{4,2,0,1,3:T(8,128)S(1)}, s32[]{:S(2)}) async-start(f32[5,2,64,8,64]{4,2,0,1,3:T(8,128)} %copy-done.1), calls=%async_computation.4 | async-start | bytes 4194304 | tf_op jit(solution)/shard_map/slice | solution.py:78
  261.7 2.8 %copy-start.10 = (s32[64]{0:T(128)S(1)}, s32[64]{0:T(128)}, u32[]{:S(2)}) copy-start(s32[64]{0:T(128)} %iota_multiply_fusion.5) | copy-start | bytes 772
  264.5 0.8 copy-start.9
  266.9 1.8 copy-start.5
Sparse Core Ops, SparseCore 0:
  191.7 51.8 all-gather.1

commit v5 on v3

--- a/solution.py
+++ b/solution.py
@@ -175,21 +175,18 @@
         ],
         axis=1,
     ).astype(jnp.bfloat16)
-    pixel_total = BANDS * PATCH * PATCH
-    payload = jnp.concatenate(
-        [
-            photos.reshape(photo_count, pixel_total),
-            jnp.pad(record, ((0, 0), (0, PATCH - record.shape[1]))),
-        ],
-        axis=1,
-    )
-    pick = slot_match.astype(jnp.bfloat16)
-    send = jnp.einsum("sp,pj->sj", pick, payload, preferred_element_type=jnp.float32).astype(
+    pixel_total = PATCH * PATCH
+    record_block = jnp.zeros((photo_count, BANDS, PATCH), jnp.bfloat16)
+    record_block = record_block.at[:, 0, : record.shape[1]].set(record)
+    payload = jnp.concatenate([photos, record_block], axis=2)
+    pick = slot_match.astype(jnp.bfloat16).reshape(owners, CAP, photo_count)
+    send = jnp.einsum("osp,pbk->osbk", pick, payload, preferred_element_type=jnp.float32).astype(
         jnp.bfloat16
     )
     got = lax.all_to_all(send, ("east", "north"), split_axis=0, concat_axis=0, tiled=True)
-    got_photos = got[:, :pixel_total]
-    record_value = got[:, pixel_total : pixel_total + 5].astype(jnp.float32)
+    got = got.reshape(slot_total, BANDS, pixel_total + PATCH)
+    got_photos = got[:, :, :pixel_total]
+    record_value = got[:, 0, pixel_total : pixel_total + 5].astype(jnp.float32)
     gain_scale = record_value[:, 0]
     block_index = record_value[:, 1].astype(jnp.int32)
     lower_row = record_value[:, 2:3]

time: 272 us -> 281 us (1.033)
  other arithmetic: 39.3 us -> 49.3 us
  waiting for transfers between devices: 121 us -> 116 us
    convert_element_type x0 -> x2, local copies, waits for them, and re-layouts: none -> 14.5 us  [the longest x1 10.9 us: body(): weighted = window_photos.astype(jnp.float32) * gain_value[:, None, :, :]]
    all_to_all x2 -> x0, local copies, waits for them, and re-layouts: 11.1 us -> none  [body(): lax.all_to_all(send, ('east', 'north'), split_axis=0, concat_axis=0, tile...]
    convert_element_type x1 -> x2, other arithmetic: 0.7 us -> 7.26 us  [the longest x1 6.49 us: body(): weighted = window_photos.astype(jnp.float32) * gain_value[:, None, :, :]]
    all_to_all x1, waiting for transfers between devices: 77.2 us -> 72.4 us  [body(): lax.all_to_all(send, ('east', 'north'), split_axis=0, concat_axis=0, tile...]
    unnamed x27 -> x61, local copies, waits for them, and re-layouts: 12.8 us -> 10.3 us
    another operation x17 -> x16, other arithmetic: 9.31 us -> 8.55 us
  transfers between devices with their start and end apart: 6 -> 6, of which waited for: 3 -> 3; matrix products, arithmetic and copies ran while one was open for 7% -> 8% of each run, Pallas kernels for 0% -> 0%
where the time goes in v5:
time: 281 us; the launch traced here: 276 us
  waiting for transfers between devices  116 us (41%)
  other arithmetic  49.3 us (18%)
  local copies, waits for them, and re-layouts  41.1 us (15%)
  matrix products  32.4 us (12%)
  starting transfers between devices  22 us (8%)
  between operations  15.2 us (5%)
    all_to_all x1, waiting for transfers between devices, body(): lax.all_to_all(send, ('east', 'north'), split_axis=0, concat_axis=0, tile...  72.4 us
    all_gather x1, waiting for transfers between devices, body(): lax.all_gather(own_levels[3][None], ('east', 'north'), axis=0, tiled=True)  41.6 us
    dot_general x16, matrix products, split_einsum(): term = jnp.einsum(spec, *pair, preferred_element_type=jnp.float32)  19 us
    ppermute x2, starting transfers between devices, add_borders(): from_low = lax.ppermute(jnp.concatenate(lows, axis=other), axis, forward)  11.8 us
    convert_element_type x1, local copies, waits for them, and re-layouts, body(): weighted = window_photos.astype(jnp.float32) * gain_value[:, None, :, :]  10.9 us
    dot_general x1, matrix products, body(): jnp.einsum('bk,kcrs->bcrs', block_match, weighted, precision=lax.Precisio...  10.8 us
    unnamed x61, local copies, waits for them, and re-layouts  10.3 us
    another operation x16, other arithmetic  8.55 us
  transfers between devices with their start and end apart: 6, of which 3 were waited for; matrix products, arithmetic and copies ran while one was open for 8% of the time, Pallas kernels for 0%

profile of v5, /device:TPU:0, one launch (start us, length us, event | category | flops | bytes accessed | tf_op | source)
XLA Modules:
  0.0 275.8 jit_solution(12628425479733143341)
XLA Ops:
  11.7 4.5 %copy.99 = bf16[32,4,16384]{2,0,1:T(8,128)(2,1)S(1)} copy(bf16[32,4,16384]{2,1,0:T(4,128)(2,1)} %param.7) | data formatting | bytes 8388608 | tf_op args[0]
  16.2 1.6 convolution_convert_fusion
  17.7 3.6 %copy.100 = bf16[16,2,4,16512]{3,2,1,0:T(4,128)(2,1)} copy(bf16[16,2,4,16512]{3,0,2,1:T(8,128)(2,1)S(1)} %convolution_convert_fusion) | data formatting | bytes 8454144 | tf_op jit(solution)/shard_map/convert_element_type | solution.py:183
  21.3 7.4 %all-to-all-start = ((bf16[16,2,4,16512]{3,2,1,0:T(4,128)(2,1)}), bf16[16,2,4,16512]{3,2,1,0:T(4,128)(2,1)}, u32[]{:S(2)}, u32[]{:S(2)}) async-start(bf16[16,2,4,16512]{3,2,1,0:T(4,128)(2,1)} %copy.100), calls=%async_computation | async-start | bytes 8454144 | tf_op jit(solution)/shard_map/all_to_all | solution.py:186
  34.6 72.4 %all-to-all-done = bf16[16,2,4,16512]{3,2,1,0:T(4,128)(2,1)} async-done(((bf16[16,2,4,16512]{3,2,1,0:T(4,128)(2,1)}), bf16[16,2,4,16512]{3,2,1,0:T(4,128)(2,1)}, u32[]{:S(2)}, u32[]{:S(2)}) %all-to-all-start) | async-done | bytes 4227104 | tf_op jit(solution)/shard_map/all_to_all | solution.py:186
  108.2 6.5 %slice_convert_fusion = f32[32,4,16384]{2,1,0:T(4,128)} fusion(bf16[32,4,16512]{2,1,0:T(4,128)(2,1)} %bitcast.8), kind=kLoop, calls=%fused_computation.56 | loop fusion | flops 2097152 | bytes 12582912 | tf_op jit(solution)/shard_map/convert_element_type | solution.py:205
  115.8 1.4 multiply_multiply_fusion
  117.3 10.9 %reshape.452 = f32[32,4,128,128]{3,2,1,0:T(8,128)} reshape(f32[32,4,16384]{2,1,0:T(4,128)} %slice_convert_fusion) | data formatting | bytes 16777216 | tf_op jit(solution)/shard_map/convert_element_type | solution.py:205
  128.2 10.8 %fusion.3 = f32[16,4,128,128]{3,0,2,1:T(8,128)S(1)} fusion(f32[32,4,128,128]{3,2,1,0:T(8,128)} %reshape.452, f32[32,128,128]{2,0,1:T(8,128)S(1)} %multiply_multiply_fusion, s32[32]{0:T(128)S(1)} %fusion.293), kind=kOutput, calls=%fused_computation.22 | convolution fusion | flops 404750848 | bytes 14680192 | tf_op jit(solution)/shard_map/bk,kcrs->bcrs/dot_general | solution.py:209
  139.0 2.5 fusion.165
  141.5 2.7 fusion.156
  145.2 2.5 fusion.1
  147.7 3.5 %fusion.29 = f32[10,260,524]{2,1,0:T(8,128)S(1)} fusion(bf16[5,524,524]{2,1,0:T(8,128)(2,1)S(1)} %get-tuple-element.26, bf16[5,524,524]{2,1,0:T(8,128)(2,1)S(1)} %get-tuple-element.25, s32[260]{0:T(512)S(1)} %copy-done.19), kind=kOutput, calls=%fused_computation.71 | convolution fusion | flops 1432720768 | bytes 10942160 | tf_op jit(solution)/shard_map/ih,chw->ciw/dot_general | solution.py:45
  152.1 2.5 fusion.21
  154.8 1.7 copy-done.2
  164.5 1.6 convolution_bitcast_fusion.3
  167.1 1.3 collective-permute-start.1
  168.5 8.8 %collective-permute-start = (f32[5,460,3]{1,2,0:T(4,128)S(1)}, f32[5,460,3]{1,2,0:T(4,128)S(1)}, u32[]{:S(2)}, u32[]{:S(2)}) collective-permute-start(f32[5,460,3]{1,2,0:T(4,128)S(1)} %pad_maximum_fusion.1), channel_id=1, source_target_pairs={{0,2},{2,4},{4,6},{6,8},{8,10},{10,12},{12,14},{1,3},{3,5},{5,7},{... | collective-permute-start | bytes 82808 | tf_op jit(solution)/shard_map/ppermute | solution.py:103
  177.3 1.7 collective-permute-done
  183.5 2.9 %pad_add_fusion.5 = f32[5,260,260]{2,1,0:T(8,128)S(1)} fusion(f32[5,260,3]{2,1,0:T(8,128)} %copy.160, f32[5,260,3]{2,1,0:T(8,128)S(1)} %copy.159, f32[260,260]{1,0:T(8,128)S(1)} %and_convert_fusion, f32[10,260,260]{2,1,0:T(8,128)} %copy-done.2), kind=kLoop, calls=%fused_computation.101 | loop fusion | flops 1352000 | bytes 4357600 | tf_op jit(solution)/shard_map/add | solution.py:117
  186.5 1.3 collective-permute-start.3
  187.9 3.0 %collective-permute-start.2 = (f32[5,3,460]{2,1,0:T(4,128)S(1)}, f32[5,3,460]{2,1,0:T(4,128)S(1)}, u32[]{:S(2)}, u32[]{:S(2)}) collective-permute-start(f32[5,3,460]{2,1,0:T(4,128)S(1)} %pad_maximum_fusion.3), channel_id=1, source_target_pairs={{0,1},{2,3},{4,5},{6,7},{8,9},{10,11},{12,13},{14,15},{16,17},{18,... | collective-permute-start | bytes 82808 | tf_op jit(solution)/shard_map/ppermute | solution.py:103
  191.0 1.3 fusion.77
  199.7 1.8 convolution_bitcast_fusion
  202.1 2.9 %fusion.38 = f32[8,512,512]{2,1,0:T(8,128)S(1)} fusion(bf16[4,512,258]{1,2,0:T(8,128)(2,1)S(1)} %get-tuple-element.44, bf16[4,512,258]{1,2,0:T(8,128)(2,1)S(1)} %get-tuple-element.43, s32[258]{0:T(512)S(1)} %copy-done.18), kind=kOutput, calls=%fused_computation.86 | convolution fusion | flops 1085300736 | bytes 10503176 | tf_op jit(solution)/shard_map/ciw,jw->cij/dot_general | solution.py:45
  205.0 3.2 %fusion.18 = bf16[4,512,512]{2,1,0:T(8,128)(2,1)} fusion(f32[8,512,512]{2,1,0:T(8,128)S(1)} %fusion.38, f32[5,512,512]{2,1,0:T(8,128)S(1)} %bitcast.147, f32[512,512]{1,0:T(8,128)S(1)} %fusion.77), kind=kLoop, calls=%fused_computation.54 | loop fusion | flops 4194304 | bytes 15728640 | tf_op jit(solution)/shard_map/convert_element_type | solution.py:262
  208.2 41.6 %all-gather.3.cloned.1.call-done = f32[80,68,68]{2,1,0:T(8,128)} async-done(((f32[5,68,68]{2,1,0:T(8,128)}), f32[80,68,68]{2,1,0:T(8,128)}) %all-gather.3.cloned.1.call-update) | async-done | bytes 1479696 | tf_op jit(solution)/shard_map/all_gather | solution.py:255
  249.8 2.8 %slice.571 = f32[8,2,5,68,64]{4,3,2,1,0:T(8,128)S(1)} slice(f32[8,2,5,68,68]{4,3,2,1,0:T(8,128)} %bitcast.148), slice={[0:8], [0:2], [0:5], [0:68], [2:66]} | slice | bytes 2785280 | tf_op jit(solution)/shard_map/slice | solution.py:127
  255.5 1.5 pad_add_fusion
  257.3 1.7 reshape.450
  258.9 1.5 slice.577
  260.6 2.0 slice.462
  (177 shorter events, 45.1 us)
Async XLA Ops:
  21.3 85.7 %all-to-all-start = ((bf16[16,2,4,16512]{3,2,1,0:T(4,128)(2,1)}), bf16[16,2,4,16512]{3,2,1,0:T(4,128)(2,1)}, u32[]{:S(2)}, u32[]{:S(2)}) async-start(bf16[16,2,4,16512]{3,2,1,0:T(4,128)(2,1)} %copy.100), calls=%async_computation | async-start | bytes 8454144 | tf_op jit(solution)/shard_map/all_to_all | solution.py:186
  28.8 221.1 %all-gather.3.cloned.1.call-start = ((), (), s32[]{:S(2)}) async-start(), calls=%async_computation.1 | async-start | bytes 3133440 | tf_op jit(solution)/shard_map/all_gather | solution.py:255
  33.8 81.0 %copy-start.10 = (f32[128,128]{1,0:T(8,128)}, f32[128,128]{1,0:T(8,128)S(1)}, u32[]{:S(2)}) copy-start(f32[128,128]{1,0:T(8,128)S(1)} %multiply_multiply_fusion.1) | copy-start | bytes 196612
  145.2 2.6 copy-start
  145.2 2.6 copy-start.19
  154.5 2.0 copy-start.2
  156.5 1.0 copy-start.22
  158.5 1.1 copy-start.6
  159.8 4.8 %copy-start.23 = (s32[68]{0:T(128)S(1)}, s32[68]{0:T(128)}, u32[]{:S(2)}) copy-start(s32[68]{0:T(128)} %iota_multiply_fusion.7) | copy-start | bytes 820
  161.8 4.8 %copy-start.11 = (f32[68,68]{1,0:T(8,128)S(1)}, f32[68,68]{1,0:T(8,128)}, u32[]{:S(2)}) copy-start(f32[68,68]{1,0:T(8,128)} %and_convert_fusion.2) | copy-start | bytes 55492
  164.5 3.9 %copy-start.12 = (f32[5,260,3]{1,2,0:T(4,128)S(1)}, f32[5,260,3]{1,2,0:T(4,128)}, u32[]{:S(2)}) copy-start(f32[5,260,3]{1,2,0:T(4,128)} %copy.119) | copy-start | bytes 46804
  166.2 14.8 %copy-start.7 = (f32[132,132]{1,0:T(8,128)S(1)}, f32[132,132]{1,0:T(8,128)}, u32[]{:S(2)}) copy-start(f32[132,132]{1,0:T(8,128)} %and_convert_fusion.1) | copy-start | bytes 209092
  166.7 14.1 %copy-start.5 = (f32[5,68,68]{2,1,0:T(8,128)}, f32[5,68,68]{2,1,0:T(8,128)S(1)}, u32[]{:S(2)}) copy-start(f32[5,68,68]{2,1,0:T(8,128)S(1)} %fusion.207) | copy-start | bytes 277444
  167.1 12.1 %collective-permute-start.1 = (f32[5,460,3]{1,2,0:T(4,128)S(1)}, f32[5,460,3]{1,2,0:T(4,128)S(1)}, u32[]{:S(2)}, u32[]{:S(2)}) collective-permute-start(f32[5,460,3]{1,2,0:T(4,128)S(1)} %pad_maximum_fusion.2), channel_id=1, source_target_pairs={{2,0},{4,2},{6,4},{8,6},{10,8},{12,10},{14,12},{3,1},{5,3},{7,5},{... | collective-permute-start | bytes 82808 | tf_op jit(solution)/shard_map/ppermute | solution.py:104
  168.5 10.5 %collective-permute-start = (f32[5,460,3]{1,2,0:T(4,128)S(1)}, f32[5,460,3]{1,2,0:T(4,128)S(1)}, u32[]{:S(2)}, u32[]{:S(2)}) collective-permute-start(f32[5,460,3]{1,2,0:T(4,128)S(1)} %pad_maximum_fusion.1), channel_id=1, source_target_pairs={{0,2},{2,4},{4,6},{6,8},{8,10},{10,12},{12,14},{1,3},{3,5},{5,7},{... | collective-permute-start | bytes 82808 | tf_op jit(solution)/shard_map/ppermute | solution.py:103
  179.0 1.3 copy-start.13
  179.3 1.4 copy-start.14
  179.7 6.7 %copy-start.8 = (f32[5,68,68]{2,1,0:T(8,128)}, f32[5,68,68]{2,1,0:T(8,128)S(1)}, u32[]{:S(2)}) copy-start(f32[5,68,68]{2,1,0:T(8,128)S(1)} %pad_add_fusion.9) | copy-start | bytes 277444
  180.5 0.8 slice-start.2
  181.2 1.1 copy-start.4
  183.5 3.0 %copy-start.16 = (f32[5,3,68]{2,1,0:T(4,128)S(1)}, f32[5,3,68]{2,1,0:T(4,128)}, u32[]{:S(2)}) copy-start(f32[5,3,68]{2,1,0:T(4,128)} %get-tuple-element.84) | copy-start | bytes 12244
  183.5 4.4 %copy-start.15 = (f32[5,3,68]{2,1,0:T(4,128)S(1)}, f32[5,3,68]{2,1,0:T(4,128)}, u32[]{:S(2)}) copy-start(f32[5,3,68]{2,1,0:T(4,128)} %get-tuple-element.83) | copy-start | bytes 12244
  186.4 7.9 %copy-start.17 = (s32[66]{0:T(128)S(1)}, s32[66]{0:T(128)}, u32[]{:S(2)}) copy-start(s32[66]{0:T(128)} %iota_multiply_fusion.6) | copy-start | bytes 796
  186.4 7.6 %copy-start.9 = (f32[5,68,68]{2,1,0:T(8,128)S(1)}, f32[5,68,68]{2,1,0:T(8,128)}, u32[]{:S(2)}) copy-start(f32[5,68,68]{2,1,0:T(8,128)} %copy-done.8) | copy-start | bytes 277444
  186.5 5.8 %collective-permute-start.3 = (f32[5,3,460]{2,1,0:T(4,128)S(1)}, f32[5,3,460]{2,1,0:T(4,128)S(1)}, u32[]{:S(2)}, u32[]{:S(2)}) collective-permute-start(f32[5,3,460]{2,1,0:T(4,128)S(1)} %pad_maximum_fusion.4), channel_id=1, source_target_pairs={{1,0},{3,2},{5,4},{7,6},{9,8},{11,10},{13,12},{15,14},{17,16},{19,... | collective-permute-start | bytes 82808 | tf_op jit(solution)/shard_map/ppermute | solution.py:104
  187.9 4.5 %collective-permute-start.2 = (f32[5,3,460]{2,1,0:T(4,128)S(1)}, f32[5,3,460]{2,1,0:T(4,128)S(1)}, u32[]{:S(2)}, u32[]{:S(2)}) collective-permute-start(f32[5,3,460]{2,1,0:T(4,128)S(1)} %pad_maximum_fusion.3), channel_id=1, source_target_pairs={{0,1},{2,3},{4,5},{6,7},{8,9},{10,11},{12,13},{14,15},{16,17},{18,... | collective-permute-start | bytes 82808 | tf_op jit(solution)/shard_map/ppermute | solution.py:103
  197.8 1.9 copy-start.18
  201.4 3.6 %slice-start = ((s8[5242880]{0:T(1024)(128)(4,1)}), s8[4194304]{0:T(1024)(128)(4,1)S(1)}, s32[]{:S(2)}) async-start(s8[5242880]{0:T(1024)(128)(4,1)} %bitcast.146), calls=%async_computation.2 | async-start | bytes 8388608
  202.1 2.9 %slice-start.1 = ((s8[5242880]{0:T(1024)(128)(4,1)}), s8[1048576]{0:T(1024)(128)(4,1)S(1)}, s32[]{:S(2)}) async-start(s8[5242880]{0:T(1024)(128)(4,1)} %bitcast.146), calls=%async_computation.3 | async-start | bytes 2097152
  249.8 2.8 %copy-start.1 = (f32[80,68,68]{2,1,0:T(8,128)S(1)}, f32[80,68,68]{2,1,0:T(8,128)}, u32[]{:S(2)}) copy-start(f32[80,68,68]{2,1,0:T(8,128)} %all-gather.3.cloned.1.call-done) | copy-start | bytes 4439044
  260.4 2.2 copy-start.3
  263.2 0.8 copy-start.21
  (1 other events, 0.7 us)
Sparse Core Ops, SparseCore 0:
  192.4 57.3 all-gather.2

commit v6 on v3

--- a/solution.py
+++ b/solution.py
@@ -255,7 +255,8 @@
             )
         )
         spill_pad = 4
-    stacked = lax.all_gather(own_levels[3][None], ("east", "north"), axis=0, tiled=True)
+    pair = lax.all_gather(own_levels[3][None], "north", axis=0, tiled=True)
+    stacked = lax.all_gather(pair, "east", axis=0, tiled=True)
     true_levels = [canvas] + add_borders(own_levels[1:])
     for depth_step in range(3):
         own_field = true_levels[depth_step]

time: 272 us -> 294 us (1.081)
  waiting for transfers between devices: 121 us -> 131 us
  local copies, waits for them, and re-layouts: 38.3 us -> 42.8 us
  other arithmetic: 39.3 us -> 43.7 us
    all_gather x1, waiting for transfers between devices: 41.6 us -> 55.1 us  [body(): stacked = lax.all_gather(pair, 'east', axis=0, tiled=True)]
    unnamed x27 -> x41, local copies, waits for them, and re-layouts: 12.8 us -> 16.6 us
where the time goes in v6:
time: 294 us; the launch traced here: 289 us
  waiting for transfers between devices  131 us (45%)
  other arithmetic  43.7 us (15%)
  local copies, waits for them, and re-layouts  42.8 us (15%)
  matrix products  32.5 us (11%)
  starting transfers between devices  21.8 us (7%)
  between operations  15.1 us (5%)
    all_to_all x1, waiting for transfers between devices, body(): lax.all_to_all(send, ('east', 'north'), split_axis=0, concat_axis=0, tile...  75.7 us
    all_gather x1, waiting for transfers between devices, body(): stacked = lax.all_gather(pair, 'east', axis=0, tiled=True)  55.1 us
    dot_general x16, matrix products, split_einsum(): term = jnp.einsum(spec, *pair, preferred_element_type=jnp.float32)  19 us
    unnamed x41, local copies, waits for them, and re-layouts  16.6 us
    ppermute x2, starting transfers between devices, add_borders(): from_low = lax.ppermute(jnp.concatenate(lows, axis=other), axis, forward)  11.8 us
    all_to_all x2, local copies, waits for them, and re-layouts, body(): lax.all_to_all(send, ('east', 'north'), split_axis=0, concat_axis=0, tile...  11.1 us
    another operation x17, other arithmetic  9.31 us
    dot_general x1, matrix products, body(): jnp.einsum('bk,kcrs->bcrs', block_match, weighted, precision=lax.Precisio...  8.72 us
  transfers between devices with their start and end apart: 6, of which 3 were waited for; matrix products, arithmetic and copies ran while one was open for 7% of the time, Pallas kernels for 0%

profile of v6, /device:TPU:0, one launch (start us, length us, event | category | flops | bytes accessed | tf_op | source)
XLA Modules:
  0.0 289.2 jit_solution(9047750859443159798)
XLA Ops:
  11.7 4.5 %copy.154 = bf16[4,8,4,16384]{3,1,2,0:T(8,128)(2,1)S(1)} copy(bf16[4,8,4,16384]{3,2,1,0:T(4,128)(2,1)} %bitcast.144) | data formatting | bytes 8388608
  16.2 3.8 %convolution_convert_fusion = bf16[32,65664]{1,0:T(8,128)(2,1)} fusion(bf16[32,5]{1,0:T(8,128)(2,1)S(1)} %copy.153, bf16[32,65536]{1,0:T(8,128)(2,1)S(1)} %bitcast.145, s32[32]{0:T(128)S(1)} %multiply_add_fusion), kind=kOutput, calls=%fused_computation | convolution fusion | flops 149189632 | bytes 8397248 | tf_op jit(solution)/shard_map/sp,pj->sj/dot_general | solution.py:187
  19.9 5.5 %all_to_all.8 = bf16[16,2,65664]{2,1,0:T(2,128)(2,1)} reshape(bf16[32,65664]{1,0:T(8,128)(2,1)} %convolution_convert_fusion) | data formatting | bytes 8404992 | tf_op jit(solution)/shard_map/all_to_all | solution.py:190
  25.4 7.4 %all-to-all-start = ((bf16[16,2,65664]{2,1,0:T(2,128)(2,1)}), bf16[16,2,65664]{2,1,0:T(2,128)(2,1)}, u32[]{:S(2)}, u32[]{:S(2)}) async-start(bf16[16,2,65664]{2,1,0:T(2,128)(2,1)} %all_to_all.8), calls=%async_computation | async-start | bytes 8404992 | tf_op jit(solution)/shard_map/all_to_all | solution.py:190
  35.0 75.7 %all-to-all-done = bf16[16,2,65664]{2,1,0:T(2,128)(2,1)} async-done(((bf16[16,2,65664]{2,1,0:T(2,128)(2,1)}), bf16[16,2,65664]{2,1,0:T(2,128)(2,1)}, u32[]{:S(2)}, u32[]{:S(2)}) %all-to-all-start) | async-done | bytes 4202528 | tf_op jit(solution)/shard_map/all_to_all | solution.py:190
  110.7 5.6 %all_to_all.10 = bf16[32,65664]{1,0:T(8,128)(2,1)} reshape(bf16[16,2,65664]{2,1,0:T(2,128)(2,1)} %all-to-all-done) | data formatting | bytes 8404992 | tf_op jit(solution)/shard_map/all_to_all | solution.py:190
  117.4 2.7 convert_bitcast_fusion
  121.9 1.5 copy.155
  123.4 8.7 %fusion.3 = f32[16,4,128,128]{3,0,2,1:T(8,128)S(1)} fusion(f32[32,4,128,128]{3,2,1,0:T(8,128)S(1)} %bitcast.141, f32[32,128,128]{2,0,1:T(8,128)S(1)} %multiply_multiply_fusion, s32[32]{0:T(128)S(1)} %fusion.292), kind=kOutput, calls=%fused_computation.22 | convolution fusion | flops 404750848 | bytes 14680192 | tf_op jit(solution)/shard_map/bk,kcrs->bcrs/dot_general | solution.py:212
  132.1 2.7 fusion.164
  134.9 2.7 fusion.155
  138.1 2.5 fusion.1
  140.7 3.5 %fusion.28 = f32[10,260,524]{2,1,0:T(8,128)S(1)} fusion(bf16[5,524,524]{2,1,0:T(8,128)(2,1)S(1)} %get-tuple-element.14, bf16[5,524,524]{2,1,0:T(8,128)(2,1)S(1)} %get-tuple-element.13, s32[260]{0:T(512)S(1)} %iota_multiply_fusion.1), kind=kOutput, calls=%fused_computation.70 | convolution fusion | flops 1432720768 | bytes 10942160 | tf_op jit(solution)/shard_map/ih,chw->ciw/dot_general | solution.py:45
  145.0 2.5 fusion.20
  147.7 1.7 copy-done.2
  157.9 1.6 convolution_bitcast_fusion.3
  161.1 1.3 collective-permute-start.1
  162.5 8.7 %collective-permute-start = (f32[5,460,3]{1,2,0:T(4,128)S(1)}, f32[5,460,3]{1,2,0:T(4,128)S(1)}, u32[]{:S(2)}, u32[]{:S(2)}) collective-permute-start(f32[5,460,3]{1,2,0:T(4,128)S(1)} %pad_maximum_fusion.1), channel_id=1, source_target_pairs={{0,2},{2,4},{4,6},{6,8},{8,10},{10,12},{12,14},{1,3},{3,5},{5,7},{... | collective-permute-start | bytes 82808 | tf_op jit(solution)/shard_map/ppermute | solution.py:103
  171.2 1.3 fusion.76
  182.3 3.1 %pad_add_fusion.5 = f32[5,260,260]{2,1,0:T(8,128)S(1)} fusion(f32[5,260,3]{2,1,0:T(8,128)} %copy.145, f32[5,260,3]{2,1,0:T(8,128)} %copy.144, f32[260,260]{1,0:T(8,128)S(1)} %and_convert_fusion, f32[10,260,260]{2,1,0:T(8,128)} %copy-done.2), kind=kLoop, calls=%fused_computation.100 | loop fusion | flops 1352000 | bytes 4357600 | tf_op jit(solution)/shard_map/add | solution.py:117
  185.5 1.3 collective-permute-start.3
  186.9 3.0 %collective-permute-start.2 = (f32[5,3,460]{2,1,0:T(4,128)S(1)}, f32[5,3,460]{2,1,0:T(4,128)S(1)}, u32[]{:S(2)}, u32[]{:S(2)}) collective-permute-start(f32[5,3,460]{2,1,0:T(4,128)S(1)} %pad_maximum_fusion.3), channel_id=1, source_target_pairs={{0,1},{2,3},{4,5},{6,7},{8,9},{10,11},{12,13},{14,15},{16,17},{18,... | collective-permute-start | bytes 82808 | tf_op jit(solution)/shard_map/ppermute | solution.py:103
  190.0 2.2 all-gather
  199.6 1.8 convolution_bitcast_fusion
  202.1 2.9 fusion.37
  205.0 3.2 %fusion.17 = bf16[4,512,512]{2,1,0:T(8,128)(2,1)} fusion(f32[8,512,512]{2,1,0:T(8,128)S(1)} %fusion.37, f32[5,512,512]{2,1,0:T(8,128)S(1)} %bitcast.140, f32[512,512]{1,0:T(8,128)S(1)} %fusion.76), kind=kLoop, calls=%fused_computation.54 | loop fusion | flops 4194304 | bytes 15728640 | tf_op jit(solution)/shard_map/convert_element_type | solution.py:266
  208.2 55.1 %all-gather.3.cloned.1.call-done = f32[16,5,68,68]{3,2,1,0:T(8,128)} async-done(((f32[2,5,68,68]{3,2,1,0:T(8,128)}), f32[16,5,68,68]{3,2,1,0:T(8,128)}) %all-gather.3.cloned.1.call-update) | async-done | bytes 1479696 | tf_op jit(solution)/shard_map/all_gather | solution.py:259
  263.3 2.8 slice.548
  268.9 1.5 pad_add_fusion
  270.7 1.6 reshape.350
  272.4 1.5 slice.554
  274.0 2.0 slice.439
  (155 shorter events, 48.0 us)
Async XLA Ops:
  25.4 85.3 %all-to-all-start = ((bf16[16,2,65664]{2,1,0:T(2,128)(2,1)}), bf16[16,2,65664]{2,1,0:T(2,128)(2,1)}, u32[]{:S(2)}, u32[]{:S(2)}) async-start(bf16[16,2,65664]{2,1,0:T(2,128)(2,1)} %all_to_all.8), calls=%async_computation | async-start | bytes 8404992 | tf_op jit(solution)/shard_map/all_to_all | solution.py:190
  32.8 230.4 %all-gather.3.cloned.1.call-start = ((), (), s32[]{:S(2)}) async-start(), calls=%async_computation.1 | async-start | bytes 3317760 | tf_op jit(solution)/shard_map/all_gather | solution.py:259
  34.9 117.7 %copy-start.7 = (f32[132,132]{1,0:T(8,128)}, f32[132,132]{1,0:T(8,128)S(1)}, u32[]{:S(2)}) copy-start(f32[132,132]{1,0:T(8,128)S(1)} %and_convert_fusion.1) | copy-start | bytes 209092
  138.1 2.5 copy-start
  147.4 2.0 copy-start.2
  160.0 19.2 %copy-start.5 = (f32[5,68,68]{2,1,0:T(8,128)}, f32[5,68,68]{2,1,0:T(8,128)S(1)}, u32[]{:S(2)}) copy-start(f32[5,68,68]{2,1,0:T(8,128)S(1)} %fusion.206) | copy-start | bytes 277444
  161.1 12.8 %collective-permute-start.1 = (f32[5,460,3]{1,2,0:T(4,128)}, f32[5,460,3]{1,2,0:T(4,128)S(1)}, u32[]{:S(2)}, u32[]{:S(2)}) collective-permute-start(f32[5,460,3]{1,2,0:T(4,128)} %pad_maximum_fusion.2), channel_id=1, source_target_pairs={{2,0},{4,2},{6,4},{8,6},{10,8},{12,10},{14,12},{3,1},{5,3},{7,5},{... | collective-permute-start | bytes 82808 | tf_op jit(solution)/shard_map/ppermute | solution.py:104
  162.5 10.5 %collective-permute-start = (f32[5,460,3]{1,2,0:T(4,128)S(1)}, f32[5,460,3]{1,2,0:T(4,128)S(1)}, u32[]{:S(2)}, u32[]{:S(2)}) collective-permute-start(f32[5,460,3]{1,2,0:T(4,128)S(1)} %pad_maximum_fusion.1), channel_id=1, source_target_pairs={{0,2},{2,4},{4,6},{6,8},{8,10},{10,12},{12,14},{1,3},{3,5},{5,7},{... | collective-permute-start | bytes 82808 | tf_op jit(solution)/shard_map/ppermute | solution.py:103
  175.9 0.7 copy-start.8
  179.2 0.9 copy-start.4
  182.3 7.7 %copy-start.6 = (f32[5,68,68]{2,1,0:T(8,128)S(1)}, f32[5,68,68]{2,1,0:T(8,128)}, u32[]{:S(2)}) copy-start(f32[5,68,68]{2,1,0:T(8,128)} %copy-done.5) | copy-start | bytes 277444
  185.5 6.7 %collective-permute-start.3 = (f32[5,3,460]{2,1,0:T(4,128)S(1)}, f32[5,3,460]{2,1,0:T(4,128)S(1)}, u32[]{:S(2)}, u32[]{:S(2)}) collective-permute-start(f32[5,3,460]{2,1,0:T(4,128)S(1)} %pad_maximum_fusion.4), channel_id=1, source_target_pairs={{1,0},{3,2},{5,4},{7,6},{9,8},{11,10},{13,12},{15,14},{17,16},{19,... | collective-permute-start | bytes 82808 | tf_op jit(solution)/shard_map/ppermute | solution.py:104
  186.9 5.4 %collective-permute-start.2 = (f32[5,3,460]{2,1,0:T(4,128)S(1)}, f32[5,3,460]{2,1,0:T(4,128)S(1)}, u32[]{:S(2)}, u32[]{:S(2)}) collective-permute-start(f32[5,3,460]{2,1,0:T(4,128)S(1)} %pad_maximum_fusion.3), channel_id=1, source_target_pairs={{0,1},{2,3},{4,5},{6,7},{8,9},{10,11},{12,13},{14,15},{16,17},{18,... | collective-permute-start | bytes 82808 | tf_op jit(solution)/shard_map/ppermute | solution.py:103
  193.6 0.9 copy-start.9
  193.9 1.5 copy-start.10
  201.4 3.5 %slice-start = ((s8[5242880]{0:T(1024)(128)(4,1)}), s8[4194304]{0:T(1024)(128)(4,1)S(1)}, s32[]{:S(2)}) async-start(s8[5242880]{0:T(1024)(128)(4,1)} %bitcast.139), calls=%async_computation.2 | async-start | bytes 8388608
  202.1 2.9 slice-start.1
  263.3 2.8 copy-start.1
  273.9 2.2 copy-start.3
  274.0 2.7 copy-start.12
  276.7 0.8 copy-start.11
Sparse Core Ops, SparseCore 0:
  192.3 70.9 all-gather.2

commit v7 on v3

--- a/solution.py
+++ b/solution.py
@@ -147,6 +147,21 @@
     )
 
 
+def doubling_gather(block, axes):
+    for axis, count in reversed(axes):
+        position = lax.axis_index(axis)
+        step = 1
+        while step < count:
+            pairs = [(i, i ^ step) for i in range(count)]
+            other = lax.ppermute(block, axis, pairs)
+            upper = (position // step) % 2 == 1
+            first = jnp.where(upper, other, block)
+            second = jnp.where(upper, block, other)
+            block = jnp.concatenate([first, second], axis=0)
+            step *= 2
+    return block
+
+
 def body(photos, footprint, placement, mask_rows, tile_scale):
     east_count = lax.axis_size("east")
     north_count = lax.axis_size("north")
@@ -255,7 +270,7 @@
             )
         )
         spill_pad = 4
-    stacked = lax.all_gather(own_levels[3][None], ("east", "north"), axis=0, tiled=True)
+    stacked = doubling_gather(own_levels[3][None], (("east", east_count), ("north", north_count)))
     true_levels = [canvas] + add_borders(own_levels[1:])
     for depth_step in range(3):
         own_field = true_levels[depth_step]

time: 272 us -> 320 us (1.18)
  waiting for transfers between devices: 121 us -> 155 us
  starting transfers between devices: 21.8 us -> 41.1 us
  between operations: 15.1 us -> 1.79 us
  other arithmetic: 39.3 us -> 43.1 us
    ppermute x0 -> x4, waiting for transfers between devices: none -> 78.6 us  [doubling_gather(): other = lax.ppermute(block, axis, pairs)]
    all_gather x1 -> x0, waiting for transfers between devices: 41.6 us -> none  [body(): lax.all_gather(own_levels[3][None], ('east', 'north'), axis=0, tiled=True)]
    ppermute x0 -> x4, starting transfers between devices: none -> 19.3 us  [doubling_gather(): other = lax.ppermute(block, axis, pairs)]
    unnamed x27 -> x35, local copies, waits for them, and re-layouts: 12.8 us -> 16.4 us
  transfers between devices with their start and end apart: 6 -> 9, of which waited for: 3 -> 6; matrix products, arithmetic and copies ran while one was open for 7% -> 6% of each run, Pallas kernels for 0% -> 0%
where the time goes in v7:
time: 320 us; the launch traced here: 315 us
  waiting for transfers between devices  155 us (48%)
  other arithmetic  43.1 us (13%)
  local copies, waits for them, and re-layouts  41.4 us (13%)
  starting transfers between devices  41.1 us (13%)
  matrix products  32.4 us (10%)
    ppermute x4, waiting for transfers between devices, doubling_gather(): other = lax.ppermute(block, axis, pairs)  78.6 us
    all_to_all x1, waiting for transfers between devices, body(): lax.all_to_all(send, ('east', 'north'), split_axis=0, concat_axis=0, tile...  75.6 us
    ppermute x4, starting transfers between devices, doubling_gather(): other = lax.ppermute(block, axis, pairs)  19.3 us
    dot_general x16, matrix products, split_einsum(): term = jnp.einsum(spec, *pair, preferred_element_type=jnp.float32)  18.9 us
    unnamed x35, local copies, waits for them, and re-layouts  16.4 us
    ppermute x2, starting transfers between devices, add_borders(): from_low = lax.ppermute(jnp.concatenate(lows, axis=other), axis, forward)  11.8 us
    all_to_all x2, local copies, waits for them, and re-layouts, body(): lax.all_to_all(send, ('east', 'north'), split_axis=0, concat_axis=0, tile...  11.1 us
    another operation x17, other arithmetic  9.25 us
  transfers between devices with their start and end apart: 9, of which 6 were waited for; matrix products, arithmetic and copies ran while one was open for 6% of the time, Pallas kernels for 0%

profile of v7, /device:TPU:0, one launch (start us, length us, event | category | flops | bytes accessed | tf_op | source)
XLA Modules:
  0.0 315.0 jit_solution(7276873758450768299)
XLA Ops:
  5.1 4.5 %copy.168 = bf16[4,8,4,16384]{3,1,2,0:T(8,128)(2,1)S(1)} copy(bf16[4,8,4,16384]{3,2,1,0:T(4,128)(2,1)} %bitcast.147) | data formatting | bytes 8388608
  9.6 3.8 %convolution_convert_fusion = bf16[32,65664]{1,0:T(8,128)(2,1)} fusion(bf16[32,5]{1,0:T(8,128)(2,1)S(1)} %copy.167, bf16[32,65536]{1,0:T(8,128)(2,1)S(1)} %bitcast.148, s32[32]{0:T(128)S(1)} %multiply_add_fusion), kind=kOutput, calls=%fused_computation | convolution fusion | flops 149189632 | bytes 8397248 | tf_op jit(solution)/shard_map/sp,pj->sj/dot_general | solution.py:202
  13.4 5.5 %all_to_all.8 = bf16[16,2,65664]{2,1,0:T(2,128)(2,1)} reshape(bf16[32,65664]{1,0:T(8,128)(2,1)} %convolution_convert_fusion) | data formatting | bytes 8404992 | tf_op jit(solution)/shard_map/all_to_all | solution.py:205
  18.9 7.4 %all-to-all-start = ((bf16[16,2,65664]{2,1,0:T(2,128)(2,1)}), bf16[16,2,65664]{2,1,0:T(2,128)(2,1)}, u32[]{:S(2)}, u32[]{:S(2)}) async-start(bf16[16,2,65664]{2,1,0:T(2,128)(2,1)} %all_to_all.8), calls=%async_computation | async-start | bytes 8404992 | tf_op jit(solution)/shard_map/all_to_all | solution.py:205
  28.6 75.6 %all-to-all-done = bf16[16,2,65664]{2,1,0:T(2,128)(2,1)} async-done(((bf16[16,2,65664]{2,1,0:T(2,128)(2,1)}), bf16[16,2,65664]{2,1,0:T(2,128)(2,1)}, u32[]{:S(2)}, u32[]{:S(2)}) %all-to-all-start) | async-done | bytes 4202528 | tf_op jit(solution)/shard_map/all_to_all | solution.py:205
  104.1 5.7 %all_to_all.10 = bf16[32,65664]{1,0:T(8,128)(2,1)} reshape(bf16[16,2,65664]{2,1,0:T(2,128)(2,1)} %all-to-all-done) | data formatting | bytes 8404992 | tf_op jit(solution)/shard_map/all_to_all | solution.py:205
  110.9 2.7 convert_bitcast_fusion
  115.4 1.5 copy.169
  116.9 8.7 %fusion.3 = f32[16,4,128,128]{3,0,2,1:T(8,128)S(1)} fusion(f32[32,4,128,128]{3,2,1,0:T(8,128)S(1)} %bitcast.146, f32[32,128,128]{2,0,1:T(8,128)S(1)} %multiply_multiply_fusion, s32[32]{0:T(128)S(1)} %fusion.292), kind=kOutput, calls=%fused_computation.22 | convolution fusion | flops 404750848 | bytes 14680192 | tf_op jit(solution)/shard_map/bk,kcrs->bcrs/dot_general | solution.py:227
  125.6 2.7 fusion.164
  128.4 2.7 fusion.155
  131.6 2.5 fusion.1
  134.1 3.5 %fusion.28 = f32[10,260,524]{2,1,0:T(8,128)S(1)} fusion(bf16[5,524,524]{2,1,0:T(8,128)(2,1)S(1)} %get-tuple-element.14, bf16[5,524,524]{2,1,0:T(8,128)(2,1)S(1)} %get-tuple-element.13, s32[260]{0:T(512)S(1)} %iota_multiply_fusion.1), kind=kOutput, calls=%fused_computation.71 | convolution fusion | flops 1432720768 | bytes 10942160 | tf_op jit(solution)/shard_map/ih,chw->ciw/dot_general | solution.py:45
  138.4 2.5 fusion.20
  141.2 1.7 copy-done.1
  150.5 1.6 convolution_bitcast_fusion.3
  154.5 8.7 %collective-permute-start = (f32[5,460,3]{1,2,0:T(4,128)S(1)}, f32[5,460,3]{1,2,0:T(4,128)S(1)}, u32[]{:S(2)}, u32[]{:S(2)}) collective-permute-start(f32[5,460,3]{1,2,0:T(4,128)S(1)} %pad_maximum_fusion.5), channel_id=1, source_target_pairs={{0,2},{2,4},{4,6},{6,8},{8,10},{10,12},{12,14},{1,3},{3,5},{5,7},{... | collective-permute-start | bytes 82808 | tf_op jit(solution)/shard_map/ppermute | solution.py:103
  174.3 3.0 pad_add_fusion.5
  178.8 3.0 collective-permute-start.2
  185.9 1.8 convolution_bitcast_fusion
  189.1 2.8 fusion.37
  192.1 10.3 %collective-permute-start.5 = (f32[2,5,68,68]{3,2,1,0:T(8,128)S(1)}, f32[2,5,68,68]{3,2,1,0:T(8,128)S(1)}, u32[]{:S(2)}, u32[]{:S(2)}) collective-permute-start(f32[2,5,68,68]{3,2,1,0:T(8,128)S(1)} %pad_maximum_fusion.3), channel_id=1, source_target_pairs={{0,2},{2,0},{4,6},{6,4},{8,10},{10,8},{12,14},{14,12},{1,3},{3,1},... | collective-permute-start | bytes 554888 | tf_op jit(solution)/shard_map/ppermute | solution.py:156
  203.2 8.3 %collective-permute-done.5 = f32[2,5,68,68]{3,2,1,0:T(8,128)S(1)} collective-permute-done((f32[2,5,68,68]{3,2,1,0:T(8,128)S(1)}, f32[2,5,68,68]{3,2,1,0:T(8,128)S(1)}, u32[]{:S(2)}, u32[]{:S(2)}) %collective-permute-start.5) | collective-permute-done | bytes 184992 | tf_op jit(solution)/shard_map/ppermute | solution.py:156
  211.9 4.5 %collective-permute-start.6 = (f32[4,5,68,68]{3,0,2,1:T(4,128)S(1)}, f32[4,5,68,68]{3,0,2,1:T(4,128)S(1)}, u32[]{:S(2)}, u32[]{:S(2)}) collective-permute-start(f32[4,5,68,68]{3,0,2,1:T(4,128)S(1)} %copy.127), channel_id=1, source_target_pairs={{0,4},{2,6},{4,0},{6,2},{8,12},{10,14},{12,8},{14,10},{1,5},{3,7},... | collective-permute-start | bytes 1109768 | tf_op jit(solution)/shard_map/ppermute | solution.py:156
  217.7 14.2 %collective-permute-done.6 = f32[4,5,68,68]{3,0,2,1:T(4,128)S(1)} collective-permute-done((f32[4,5,68,68]{3,0,2,1:T(4,128)S(1)}, f32[4,5,68,68]{3,0,2,1:T(4,128)S(1)}, u32[]{:S(2)}, u32[]{:S(2)}) %collective-permute-start.6) | collective-permute-done | bytes 369952 | tf_op jit(solution)/shard_map/ppermute | solution.py:156
  233.5 4.4 %collective-permute-start.7 = (f32[8,5,68,68]{3,0,2,1:T(8,128)}, f32[8,5,68,68]{3,0,2,1:T(8,128)S(1)}, u32[]{:S(2)}, u32[]{:S(2)}) collective-permute-start(f32[8,5,68,68]{3,0,2,1:T(8,128)} %copy.130), channel_id=1, source_target_pairs={{0,8},{2,10},{4,12},{6,14},{8,0},{10,2},{12,4},{14,6},{1,9},{3,11}... | collective-permute-start | bytes 2219528 | tf_op jit(solution)/shard_map/ppermute | solution.py:156
  238.0 3.2 %fusion.17 = bf16[4,512,512]{2,1,0:T(8,128)(2,1)} fusion(f32[8,512,512]{2,1,0:T(8,128)S(1)} %fusion.37, f32[5,512,512]{2,1,0:T(8,128)S(1)} %bitcast.143, f32[512,512]{1,0:T(8,128)S(1)} %fusion.76), kind=kLoop, calls=%fused_computation.54 | loop fusion | flops 4194304 | bytes 15728640 | tf_op jit(solution)/shard_map/convert_element_type | solution.py:280
  241.2 56.2 %collective-permute-done.7 = f32[8,5,68,68]{3,0,2,1:T(8,128)S(1)} collective-permute-done((f32[8,5,68,68]{3,0,2,1:T(8,128)}, f32[8,5,68,68]{3,0,2,1:T(8,128)S(1)}, u32[]{:S(2)}, u32[]{:S(2)}) %collective-permute-start.7) | collective-permute-done | bytes 739872 | tf_op jit(solution)/shard_map/ppermute | solution.py:156
  301.6 1.5 pad_add_fusion
  303.3 1.7 reshape.350
  305.0 1.5 slice.554
  306.6 2.0 slice.439
  (164 shorter events, 53.6 us)
Async XLA Ops:
  18.9 85.3 %all-to-all-start = ((bf16[16,2,65664]{2,1,0:T(2,128)(2,1)}), bf16[16,2,65664]{2,1,0:T(2,128)(2,1)}, u32[]{:S(2)}, u32[]{:S(2)}) async-start(bf16[16,2,65664]{2,1,0:T(2,128)(2,1)} %all_to_all.8), calls=%async_computation | async-start | bytes 8404992 | tf_op jit(solution)/shard_map/all_to_all | solution.py:205
  131.6 2.5 copy-start
  140.9 2.0 copy-start.1
  153.1 12.8 %collective-permute-start.1 = (f32[5,460,3]{1,2,0:T(4,128)S(1)}, f32[5,460,3]{1,2,0:T(4,128)S(1)}, u32[]{:S(2)}, u32[]{:S(2)}) collective-permute-start(f32[5,460,3]{1,2,0:T(4,128)S(1)} %pad_maximum_fusion.6), channel_id=1, source_target_pairs={{2,0},{4,2},{6,4},{8,6},{10,8},{12,10},{14,12},{3,1},{5,3},{7,5},{... | collective-permute-start | bytes 82808 | tf_op jit(solution)/shard_map/ppermute | solution.py:104
  154.5 10.5 %collective-permute-start = (f32[5,460,3]{1,2,0:T(4,128)S(1)}, f32[5,460,3]{1,2,0:T(4,128)S(1)}, u32[]{:S(2)}, u32[]{:S(2)}) collective-permute-start(f32[5,460,3]{1,2,0:T(4,128)S(1)} %pad_maximum_fusion.5), channel_id=1, source_target_pairs={{0,2},{2,4},{4,6},{6,8},{8,10},{10,12},{12,14},{1,3},{3,5},{5,7},{... | collective-permute-start | bytes 82808 | tf_op jit(solution)/shard_map/ppermute | solution.py:103
  167.9 0.7 copy-start.5
  172.0 0.9 copy-start.3
  174.3 8.5 %copy-start.6 = (f32[5,68,68]{2,1,0:T(8,128)S(1)}, f32[5,68,68]{2,1,0:T(8,128)}, u32[]{:S(2)}) copy-start(f32[5,68,68]{2,1,0:T(8,128)} %copy-done.5) | copy-start | bytes 277444
  174.3 8.8 %copy-start.4 = (f32[5,132,132]{2,1,0:T(8,128)S(1)}, f32[5,132,132]{2,1,0:T(8,128)}, u32[]{:S(2)}) copy-start(f32[5,132,132]{2,1,0:T(8,128)} %copy-done.3) | copy-start | bytes 1045444
  177.4 4.5 %collective-permute-start.3 = (f32[5,3,460]{2,1,0:T(4,128)S(1)}, f32[5,3,460]{2,1,0:T(4,128)S(1)}, u32[]{:S(2)}, u32[]{:S(2)}) collective-permute-start(f32[5,3,460]{2,1,0:T(4,128)S(1)} %pad_maximum_fusion.8), channel_id=1, source_target_pairs={{1,0},{3,2},{5,4},{7,6},{9,8},{11,10},{13,12},{15,14},{17,16},{19,... | collective-permute-start | bytes 82808 | tf_op jit(solution)/shard_map/ppermute | solution.py:104
  178.8 3.9 %collective-permute-start.2 = (f32[5,3,460]{2,1,0:T(4,128)S(1)}, f32[5,3,460]{2,1,0:T(4,128)S(1)}, u32[]{:S(2)}, u32[]{:S(2)}) collective-permute-start(f32[5,3,460]{2,1,0:T(4,128)S(1)} %pad_maximum_fusion.7), channel_id=1, source_target_pairs={{0,1},{2,3},{4,5},{6,7},{8,9},{10,11},{12,13},{14,15},{16,17},{18,... | collective-permute-start | bytes 82808 | tf_op jit(solution)/shard_map/ppermute | solution.py:103
  181.8 10.2 %collective-permute-start.4 = (f32[1,5,68,68]{3,2,1,0:T(8,128)S(1)}, f32[1,5,68,68]{3,2,1,0:T(8,128)S(1)}, u32[]{:S(2)}, u32[]{:S(2)}) collective-permute-start(f32[1,5,68,68]{3,2,1,0:T(8,128)S(1)} %fusion.481), channel_id=1, source_target_pairs={{0,1},{1,0},{2,3},{3,2},{4,5},{5,4},{6,7},{7,6},{8,9},{9,8},{10,11... | collective-permute-start | bytes 277448 | tf_op jit(solution)/shard_map/ppermute | solution.py:156
  183.9 0.7 copy-start.7
  192.1 19.4 %collective-permute-start.5 = (f32[2,5,68,68]{3,2,1,0:T(8,128)S(1)}, f32[2,5,68,68]{3,2,1,0:T(8,128)S(1)}, u32[]{:S(2)}, u32[]{:S(2)}) collective-permute-start(f32[2,5,68,68]{3,2,1,0:T(8,128)S(1)} %pad_maximum_fusion.3), channel_id=1, source_target_pairs={{0,2},{2,0},{4,6},{6,4},{8,10},{10,8},{12,14},{14,12},{1,3},{3,1},... | collective-permute-start | bytes 554888 | tf_op jit(solution)/shard_map/ppermute | solution.py:156
  211.9 20.0 %collective-permute-start.6 = (f32[4,5,68,68]{3,0,2,1:T(4,128)S(1)}, f32[4,5,68,68]{3,0,2,1:T(4,128)S(1)}, u32[]{:S(2)}, u32[]{:S(2)}) collective-permute-start(f32[4,5,68,68]{3,0,2,1:T(4,128)S(1)} %copy.127), channel_id=1, source_target_pairs={{0,4},{2,6},{4,0},{6,2},{8,12},{10,14},{12,8},{14,10},{1,5},{3,7},... | collective-permute-start | bytes 1109768 | tf_op jit(solution)/shard_map/ppermute | solution.py:156
  216.5 21.5 %slice-start = ((s8[5242880]{0:T(1024)(128)(4,1)}), s8[4194304]{0:T(1024)(128)(4,1)S(1)}, s32[]{:S(2)}) async-start(s8[5242880]{0:T(1024)(128)(4,1)} %bitcast.142), calls=%async_computation.1 | async-start | bytes 8388608
  217.7 20.2 %slice-start.1 = ((s8[5242880]{0:T(1024)(128)(4,1)}), s8[1048576]{0:T(1024)(128)(4,1)S(1)}, s32[]{:S(2)}) async-start(s8[5242880]{0:T(1024)(128)(4,1)} %bitcast.142), calls=%async_computation.2 | async-start | bytes 2097152
  233.5 63.8 %collective-permute-start.7 = (f32[8,5,68,68]{3,0,2,1:T(8,128)}, f32[8,5,68,68]{3,0,2,1:T(8,128)S(1)}, u32[]{:S(2)}, u32[]{:S(2)}) collective-permute-start(f32[8,5,68,68]{3,0,2,1:T(8,128)} %copy.130), channel_id=1, source_target_pairs={{0,8},{2,10},{4,12},{6,14},{8,0},{10,2},{12,4},{14,6},{1,9},{3,11}... | collective-permute-start | bytes 2219528 | tf_op jit(solution)/shard_map/ppermute | solution.py:156
  306.5 2.2 copy-start.2
  306.6 2.7 copy-start.9
  309.3 0.8 copy-start.8

commit v8 on v3

--- a/solution.py
+++ b/solution.py
@@ -209,21 +209,20 @@
     block_match = (block_index[None, :] == jnp.arange(BLOCKS, dtype=jnp.int32)[:, None]).astype(
         jnp.float32
     )
-    band_sums = jnp.einsum(
-        "bk,kcrs->bcrs",
-        block_match,
-        weighted,
-        precision=lax.Precision.HIGHEST,
-        preferred_element_type=jnp.float32,
-    )
-    weight_sums = jnp.einsum(
-        "bk,krs->brs",
-        block_match,
-        weight,
-        precision=lax.Precision.HIGHEST,
-        preferred_element_type=jnp.float32,
-    )
-    summed = jnp.concatenate([band_sums, weight_sums[:, None]], axis=1)
+    contribution = jnp.concatenate([weighted, weight[:, None]], axis=1)
+    pieces = []
+    remainder = contribution
+    for _ in range(2):
+        spread_part = remainder * 65537.0
+        high = spread_part - (spread_part - remainder)
+        pieces.append(high)
+        remainder = remainder - high
+    pieces.append(remainder)
+    stacked_pieces = jnp.concatenate(pieces, axis=0).astype(jnp.bfloat16)
+    match_pieces = jnp.concatenate([block_match] * 3, axis=1).astype(jnp.bfloat16)
+    summed = jnp.einsum(
+        "bk,kcrs->bcrs", match_pieces, stacked_pieces, preferred_element_type=jnp.float32
+    )
     side_blocks = TILE // PATCH
     strips = []
     for block_row in range(side_blocks):

time: 272 us -> 280 us (1.029)
  waiting for transfers between devices: 121 us -> 96.6 us
  other arithmetic: 39.3 us -> 58.7 us
  local copies, waits for them, and re-layouts: 38.3 us -> 55.2 us
  matrix products: 32.4 us -> 29.4 us
    all_gather x1, waiting for transfers between devices: 41.6 us -> 10.9 us  [body(): lax.all_gather(own_levels[3][None], ('east', 'north'), axis=0, tiled=True)]
    ppermute x2, waiting for transfers between devices: 0.01 us -> 12 us  [add_borders(): from_high = lax.ppermute(jnp.concatenate(highs, axis=other), axis, backward)]
    mul x0 -> x2, other arithmetic: none -> 8.93 us  [the longest x1 8.33 us: body(): weighted = window_photos.astype(jnp.float32) * gain_value[:, None, :, :]]
    another operation x17 -> x18, other arithmetic: 9.31 us -> 16.3 us
    unnamed x27 -> x51, local copies, waits for them, and re-layouts: 12.8 us -> 19.5 us
    concatenate x2 -> x0, other arithmetic: 5.48 us -> none  [body(): summed = jnp.concatenate([band_sums, weight_sums[:, None]], axis=1)]
    slice x0 -> x1, local copies, waits for them, and re-layouts: none -> 4.9 us  [body(): summed[block_row * side_blocks + block_col]]
    all_to_all x1, waiting for transfers between devices: 77.2 us -> 73.7 us  [body(): lax.all_to_all(send, ('east', 'north'), split_axis=0, concat_axis=0, tile...]
  transfers between devices with their start and end apart: 6 -> 6, of which waited for: 3 -> 4; matrix products, arithmetic and copies ran while one was open for 7% -> 13% of each run, Pallas kernels for 0% -> 0%
where the time goes in v8:
time: 280 us; the launch traced here: 275 us
  waiting for transfers between devices  96.6 us (34%)
  other arithmetic  58.7 us (21%)
  local copies, waits for them, and re-layouts  55.2 us (20%)
  matrix products  29.4 us (10%)
  starting transfers between devices  19.6 us (7%)
  between operations  15.1 us (5%)
    all_to_all x1, waiting for transfers between devices, body(): lax.all_to_all(send, ('east', 'north'), split_axis=0, concat_axis=0, tile...  73.7 us
    unnamed x51, local copies, waits for them, and re-layouts  19.5 us
    dot_general x16, matrix products, split_einsum(): term = jnp.einsum(spec, *pair, preferred_element_type=jnp.float32)  18.8 us
    another operation x18, other arithmetic  16.3 us
    ppermute x2, waiting for transfers between devices, add_borders(): from_high = lax.ppermute(jnp.concatenate(highs, axis=other), axis, backward)  12 us
    all_to_all x2, local copies, waits for them, and re-layouts, body(): lax.all_to_all(send, ('east', 'north'), split_axis=0, concat_axis=0, tile...  10.9 us
    all_gather x1, waiting for transfers between devices, body(): lax.all_gather(own_levels[3][None], ('east', 'north'), axis=0, tiled=True)  10.9 us
    ppermute x2, starting transfers between devices, add_borders(): from_low = lax.ppermute(jnp.concatenate(lows, axis=other), axis, forward)  9.39 us
  transfers between devices with their start and end apart: 6, of which 4 were waited for; matrix products, arithmetic and copies ran while one was open for 13% of the time, Pallas kernels for 0%

profile of v8, /device:TPU:0, one launch (start us, length us, event | category | flops | bytes accessed | tf_op | source)
XLA Modules:
  0.0 274.5 jit_solution(18296623130474299066)
XLA Ops:
  11.7 4.5 %copy.152 = bf16[4,8,4,16384]{3,1,2,0:T(8,128)(2,1)S(1)} copy(bf16[4,8,4,16384]{3,2,1,0:T(4,128)(2,1)} %bitcast.138) | data formatting | bytes 8388608
  16.2 3.7 %convolution_convert_fusion = bf16[32,65664]{1,0:T(8,128)(2,1)} fusion(bf16[32,5]{1,0:T(8,128)(2,1)S(1)} %copy.151, bf16[32,65536]{1,0:T(8,128)(2,1)S(1)} %bitcast.139, s32[32]{0:T(128)S(1)} %multiply_add_fusion), kind=kOutput, calls=%fused_computation | convolution fusion | flops 149189632 | bytes 8397248 | tf_op jit(solution)/shard_map/sp,pj->sj/dot_general | solution.py:187
  19.9 5.5 %all_to_all.8 = bf16[16,2,65664]{2,1,0:T(2,128)(2,1)} reshape(bf16[32,65664]{1,0:T(8,128)(2,1)} %convolution_convert_fusion) | data formatting | bytes 8404992 | tf_op jit(solution)/shard_map/all_to_all | solution.py:190
  25.4 7.4 %all-to-all-start = ((bf16[16,2,65664]{2,1,0:T(2,128)(2,1)}), bf16[16,2,65664]{2,1,0:T(2,128)(2,1)}, u32[]{:S(2)}, u32[]{:S(2)}) async-start(bf16[16,2,65664]{2,1,0:T(2,128)(2,1)} %all_to_all.8), calls=%async_computation | async-start | bytes 8404992 | tf_op jit(solution)/shard_map/all_to_all | solution.py:190
  37.0 73.7 %all-to-all-done = bf16[16,2,65664]{2,1,0:T(2,128)(2,1)} async-done(((bf16[16,2,65664]{2,1,0:T(2,128)(2,1)}), bf16[16,2,65664]{2,1,0:T(2,128)(2,1)}, u32[]{:S(2)}, u32[]{:S(2)}) %all-to-all-start) | async-done | bytes 4202528 | tf_op jit(solution)/shard_map/all_to_all | solution.py:190
  110.6 5.5 %all_to_all.10 = bf16[32,65664]{1,0:T(8,128)(2,1)} reshape(bf16[16,2,65664]{2,1,0:T(2,128)(2,1)} %all-to-all-done) | data formatting | bytes 8404992 | tf_op jit(solution)/shard_map/all_to_all | solution.py:190
  116.8 2.7 convert_bitcast_fusion
  121.3 4.8 %copy.153 = f32[4,8,512,128]{3,2,1,0:T(8,128)} copy(f32[4,8,512,128]{3,1,2,0:T(8,128)S(1)} %convert_bitcast_fusion) | data formatting | bytes 16777216
  126.0 8.3 %copy_multiply_fusion = f32[32,4,128,128]{3,0,2,1:T(8,128)S(1)} fusion(f32[32,4,128,128]{3,2,1,0:T(8,128)} %bitcast.135, f32[32,128,128]{2,0,1:T(8,128)S(1)} %multiply_multiply_fusion), kind=kLoop, calls=%fused_computation.20 | loop fusion | flops 2097152 | bytes 18874368 | tf_op jit(solution)/shard_map/mul | solution.py:208
  134.4 7.2 %fusion.7 = (bf16[32,5,128,128]{3,0,2,1:T(8,128)(2,1)}, bf16[32,5,128,128]{3,0,2,1:T(8,128)(2,1)}, bf16[32,5,128,128]{3,0,2,1:T(8,128)(2,1)}) fusion(f32[32,1,128,128]{3,0,2,1:T(8,128)S(1)} %broadcast_multiply_fusion, f32[32,4,128,128]{3,0,2,1:T(8,128)S(1)} %copy_multiply_fusion), kind=kLoop, calls=%fused_computation.10 | loop fusion | flops 31457280 | bytes 26214400 | tf_op jit(solution)/shard_map/convert.35
  141.5 6.9 %fusion = f32[16,5,128,128]{3,0,2,1:T(8,128)S(1)} fusion(bf16[32,5,128,128]{3,0,2,1:T(8,128)(2,1)} %get-tuple-element.13, bf16[32,5,128,128]{3,0,2,1:T(8,128)(2,1)} %get-tuple-element.12, bf16[32,5,128,128]{3,0,2,1:T(8,128)(2,1)} %get-tuple-element.11, pred[16,32]{1,0:T(8,128)(4,1)S(1)} %iota_compare_fusion.4), kind=kOutput, calls=%fused_computation.1 | convolution fusion | flops 298850304 | bytes 20972032 | tf_op jit(solution)/shard_map/bk,kcrs->bcrs/dot_general | solution.py:223
  148.4 4.9 %fusion.458 = (f32[1,5,128,128]{3,0,2,1:T(1,128)S(1)}, f32[1,5,128,128]{3,0,2,1:T(1,128)S(1)}, f32[1,5,128,128]{3,0,2,1:T(1,128)S(1)}, f32[1,5,128,128]{3,0,2,1:...) fusion(f32[16,5,128,128]{3,0,2,1:T(8,128)S(1)} %fusion), kind=kLoop, calls=%fused_computation.562 | loop fusion | bytes 10485760 | tf_op jit(solution)/shard_map/slice | solution.py:231
  153.3 3.8 %maximum_maximum_fusion = f32[5,512,512]{2,1,0:T(8,128)S(1)} fusion(f32[5,128,128]{2,1,0:T(8,128)} %bitcast.154, f32[5,128,128]{2,1,0:T(8,128)} %bitcast.155, f32[5,128,128]{2,1,0:T(8,128)S(1)} %bitcast.141, f32[5,128,128]{2,1,0:T(8,128)S(1)} %bitcast.142, f32[5,128,128]{2,1,0:T(8,128)S(1)} %bitcast.143, f32[5,128,128]{2,1,0:T(8,128)S(1)} %bitcast.144, ...), kind=kLoop, calls=%fused_computation.27 | loop fusion | flops 19660800 | bytes 10485760 | tf_op jit(solution)/shard_map/concatenate | solution.py:235
  157.2 2.5 fusion.12
  159.7 3.5 %fusion.35 = f32[10,260,524]{2,1,0:T(8,128)S(1)} fusion(bf16[5,524,524]{2,1,0:T(8,128)(2,1)S(1)} %get-tuple-element.17, bf16[5,524,524]{2,1,0:T(8,128)(2,1)S(1)} %get-tuple-element.16, s32[260]{0:T(512)S(1)} %iota_multiply_fusion.1), kind=kOutput, calls=%fused_computation.49 | convolution fusion | flops 1432720768 | bytes 10942160 | tf_op jit(solution)/shard_map/ih,chw->ciw/dot_general | solution.py:45
  164.0 2.5 fusion.29
  166.8 1.7 copy-done.3
  177.6 8.1 %collective-permute-start = (f32[5,460,3]{1,2,0:T(4,128)S(1)}, f32[5,460,3]{1,2,0:T(4,128)S(1)}, u32[]{:S(2)}, u32[]{:S(2)}) collective-permute-start(f32[5,460,3]{1,2,0:T(4,128)S(1)} %pad_maximum_fusion.1), channel_id=1, source_target_pairs={{0,2},{2,4},{4,6},{6,8},{8,10},{10,12},{12,14},{1,3},{3,5},{5,7},{... | collective-permute-start | bytes 82808 | tf_op jit(solution)/shard_map/ppermute | solution.py:103
  191.0 11.6 %collective-permute-done.1 = f32[5,460,3]{1,2,0:T(4,128)S(1)} collective-permute-done((f32[5,460,3]{1,2,0:T(4,128)S(1)}, f32[5,460,3]{1,2,0:T(4,128)S(1)}, u32[]{:S(2)}, u32[]{:S(2)}) %collective-permute-start.1) | collective-permute-done | bytes 27632 | tf_op jit(solution)/shard_map/ppermute | solution.py:104
  204.3 3.2 %pad_add_fusion.5 = f32[5,260,260]{2,1,0:T(8,128)S(1)} fusion(f32[5,260,3]{2,1,0:T(8,128)} %copy.143, f32[5,260,3]{2,1,0:T(8,128)} %copy.142, f32[260,260]{1,0:T(8,128)} %copy-done.5, f32[10,260,260]{2,1,0:T(8,128)} %copy-done.3), kind=kLoop, calls=%fused_computation.80 | loop fusion | flops 1352000 | bytes 4357600 | tf_op jit(solution)/shard_map/add | solution.py:117
  211.1 1.4 pad_add_fusion.7
  216.6 1.3 collective-permute-start.2
  218.0 1.3 collective-permute-start.3
  219.3 1.3 fusion.80
  227.1 1.8 convolution_bitcast_fusion
  229.6 2.8 %fusion.44 = f32[8,512,512]{2,1,0:T(8,128)S(1)} fusion(bf16[4,512,258]{1,2,0:T(8,128)(2,1)S(1)} %get-tuple-element.35, bf16[4,512,258]{1,2,0:T(8,128)(2,1)S(1)} %get-tuple-element.34, s32[258]{0:T(512)S(1)} %iota_multiply_fusion), kind=kOutput, calls=%fused_computation.64 | convolution fusion | flops 1085300736 | bytes 10503176 | tf_op jit(solution)/shard_map/ciw,jw->cij/dot_general | solution.py:45
  232.5 3.2 %fusion.27 = bf16[4,512,512]{2,1,0:T(8,128)(2,1)} fusion(f32[8,512,512]{2,1,0:T(8,128)S(1)} %fusion.44, f32[5,512,512]{2,1,0:T(8,128)S(1)} %bitcast.134, f32[512,512]{1,0:T(8,128)S(1)} %fusion.80), kind=kLoop, calls=%fused_computation.37 | loop fusion | flops 4194304 | bytes 15728640 | tf_op jit(solution)/shard_map/convert_element_type | solution.py:264
  235.7 10.9 %all-gather.3.cloned.1.call-done = f32[80,68,68]{2,1,0:T(8,128)} async-done(((f32[5,68,68]{2,1,0:T(8,128)}), f32[80,68,68]{2,1,0:T(8,128)}) %all-gather.3.cloned.1.call-update) | async-done | bytes 1479696 | tf_op jit(solution)/shard_map/all_gather | solution.py:257
  246.5 3.5 %fusion.459 = (f32[7,2,5,68,2]{4,3,2,1,0:T(8,128)S(1)}, f32[7,2,5,68,2]{4,3,2,1,0:T(8,128)S(1)}) fusion(f32[8,2,5,68,68]{4,3,2,1,0:T(8,128)} %bitcast.136), kind=kLoop, calls=%fused_computation.563 | loop fusion | bytes 152320 | tf_op jit(solution)/shard_map/slice | solution.py:136
  252.9 1.5 pad_add_fusion
  254.6 1.9 reshape.352
  264.2 2.0 fusion.121
  (167 shorter events, 54.6 us)
Async XLA Ops:
  25.4 85.3 %all-to-all-start = ((bf16[16,2,65664]{2,1,0:T(2,128)(2,1)}), bf16[16,2,65664]{2,1,0:T(2,128)(2,1)}, u32[]{:S(2)}, u32[]{:S(2)}) async-start(bf16[16,2,65664]{2,1,0:T(2,128)(2,1)} %all_to_all.8), calls=%async_computation | async-start | bytes 8404992 | tf_op jit(solution)/shard_map/all_to_all | solution.py:190
  32.8 213.7 %all-gather.3.cloned.1.call-start = ((), (), s32[]{:S(2)}) async-start(), calls=%async_computation.1 | async-start | bytes 3133440 | tf_op jit(solution)/shard_map/all_gather | solution.py:257
  37.0 129.5 %copy-start.5 = (f32[260,260]{1,0:T(8,128)}, f32[260,260]{1,0:T(8,128)S(1)}, u32[]{:S(2)}) copy-start(f32[260,260]{1,0:T(8,128)S(1)} %and_convert_fusion) | copy-start | bytes 811204
  157.2 2.5 copy-start
  166.5 2.0 copy-start.3
  168.5 0.8 copy-start.15
  170.3 1.1 copy-start.10
  171.5 1.5 copy-start.17
  174.0 28.6 %copy-start.9 = (f32[10,68,68]{2,1,0:T(8,128)}, f32[10,68,68]{2,1,0:T(8,128)S(1)}, u32[]{:S(2)}) copy-start(f32[10,68,68]{2,1,0:T(8,128)S(1)} %fusion.143) | copy-start | bytes 554884
  174.0 15.7 %copy-start.8 = (f32[5,68,68]{2,1,0:T(8,128)}, f32[5,68,68]{2,1,0:T(8,128)S(1)}, u32[]{:S(2)}) copy-start(f32[5,68,68]{2,1,0:T(8,128)S(1)} %fusion.193) | copy-start | bytes 277444
  177.6 12.1 %collective-permute-start = (f32[5,460,3]{1,2,0:T(4,128)S(1)}, f32[5,460,3]{1,2,0:T(4,128)S(1)}, u32[]{:S(2)}, u32[]{:S(2)}) collective-permute-start(f32[5,460,3]{1,2,0:T(4,128)S(1)} %pad_maximum_fusion.1), channel_id=1, source_target_pairs={{0,2},{2,4},{4,6},{6,8},{8,10},{10,12},{12,14},{1,3},{3,5},{5,7},{... | collective-permute-start | bytes 82808 | tf_op jit(solution)/shard_map/ppermute | solution.py:103
  188.4 14.2 %collective-permute-start.1 = (f32[5,460,3]{1,2,0:T(4,128)S(1)}, f32[5,460,3]{1,2,0:T(4,128)S(1)}, u32[]{:S(2)}, u32[]{:S(2)}) collective-permute-start(f32[5,460,3]{1,2,0:T(4,128)S(1)} %pad_maximum_fusion.2), channel_id=1, source_target_pairs={{2,0},{4,2},{6,4},{8,6},{10,8},{12,10},{14,12},{3,1},{5,3},{7,5},{... | collective-permute-start | bytes 82808 | tf_op jit(solution)/shard_map/ppermute | solution.py:104
  189.8 14.6 %copy-start.11 = (f32[5,460,3]{1,2,0:T(4,128)}, f32[5,460,3]{1,2,0:T(4,128)S(1)}, u32[]{:S(2)}) copy-start(f32[5,460,3]{1,2,0:T(4,128)S(1)} %collective-permute-done) | copy-start | bytes 82804
  202.6 0.6 copy-start.12
  212.5 0.9 copy-start.6
  213.3 7.8 %copy-start.7 = (f32[5,132,132]{2,1,0:T(8,128)S(1)}, f32[5,132,132]{2,1,0:T(8,128)}, u32[]{:S(2)}) copy-start(f32[5,132,132]{2,1,0:T(8,128)} %copy-done.6) | copy-start | bytes 1045444
  216.6 4.0 %collective-permute-start.2 = (f32[5,3,460]{2,1,0:T(4,128)S(1)}, f32[5,3,460]{2,1,0:T(4,128)S(1)}, u32[]{:S(2)}, u32[]{:S(2)}) collective-permute-start(f32[5,3,460]{2,1,0:T(4,128)S(1)} %pad_maximum_fusion.3), channel_id=1, source_target_pairs={{0,1},{2,3},{4,5},{6,7},{8,9},{10,11},{12,13},{14,15},{16,17},{18,... | collective-permute-start | bytes 82808 | tf_op jit(solution)/shard_map/ppermute | solution.py:103
  218.0 3.1 %collective-permute-start.3 = (f32[5,3,460]{2,1,0:T(4,128)S(1)}, f32[5,3,460]{2,1,0:T(4,128)S(1)}, u32[]{:S(2)}, u32[]{:S(2)}) collective-permute-start(f32[5,3,460]{2,1,0:T(4,128)S(1)} %pad_maximum_fusion.4), channel_id=1, source_target_pairs={{1,0},{3,2},{5,4},{7,6},{9,8},{11,10},{13,12},{15,14},{17,16},{19,... | collective-permute-start | bytes 82808 | tf_op jit(solution)/shard_map/ppermute | solution.py:104
  220.6 1.8 copy-start.13
  228.9 3.5 %slice-start = ((s8[5242880]{0:T(1024)(128)(4,1)}), s8[4194304]{0:T(1024)(128)(4,1)S(1)}, s32[]{:S(2)}) async-start(s8[5242880]{0:T(1024)(128)(4,1)} %bitcast.133), calls=%async_computation.2 | async-start | bytes 8388608
  229.6 2.9 %slice-start.1 = ((s8[5242880]{0:T(1024)(128)(4,1)}), s8[1048576]{0:T(1024)(128)(4,1)S(1)}, s32[]{:S(2)}) async-start(s8[5242880]{0:T(1024)(128)(4,1)} %bitcast.133), calls=%async_computation.3 | async-start | bytes 2097152
  246.5 3.5 %copy-start.2 = (f32[80,68,68]{2,1,0:T(8,128)S(1)}, f32[80,68,68]{2,1,0:T(8,128)}, u32[]{:S(2)}) copy-start(f32[80,68,68]{2,1,0:T(8,128)} %all-gather.3.cloned.1.call-done) | copy-start | bytes 4439044
  254.6 1.9 copy-start.1
  256.5 1.5 copy-start.4
  256.5 2.1 copy-start.16
  258.6 0.8 copy-start.14
  260.1 2.4 slice-start.2
Sparse Core Ops, SparseCore 0:
  189.9 56.6 all-gather.2
